TPU v7x, 256 devices: a whole 4x4x8 slice. The times are simulated.
256 devices in a mesh: wave: 8 (over z_lo, core), tile: 32 (over x, z_hi, y).
Axes of the slice: x: 4, y: 4, z: 8 (z_hi: 2, z_lo: 4; z = z_hi * 4 + z_lo), core: 2. Of those that a mesh axis runs over, the one named last changes fastest.
Arguments:
- thickness: float32 [32, 256, 256], P('tile'), may hold values from 0 to 1
- illumination: float32 [16, 2, 256, 256], P('wave'), may hold values from -6 to 6
- absorb: float32 [16], P('wave'), may hold values from 0.1 to 0.8
- phases: float32 [16], P('wave'), may hold values from 0.1 to 0.8
- amplitudes: bfloat16 [32, 6, 16, 256, 256], P('tile', None, 'wave'), may hold values from 0.049804688 to 0.5
- positions: int32 [32, 6, 2], P('tile'), may hold values from 0 to 255, as said below
- batch_order: int32 [32, 6], P('tile'), may hold values from 0 to 5, each once within a row
- live_slots: int32 [32, 3, 2], P('tile'), may hold values from 0 to 1, as said below
Outputs:
- thickness_new: float32 [32, 256, 256], P('tile')
Inputs may be any that keep to these rules, and one draw needn't show every extreme that they name: `positions`: offsets inside the tile that owns the pattern; the 256 x 256 window from every slot's corner lies inside the object. `live_slots`: in every batch at least one tile has its slot 0 live.
All inputs are finite; a program needn't handle non-finite values.
Results may differ from a plain program's by a relative error of at most 0.0003.
Values sent between devices are 32-bit elements; how exact they have to be, the bound alone decides.
No kernel may reach another device: no remote copies, remote signals or barrier semaphores. Data moves between devices by JAX's collectives and lax.ppermute only.
A program may use at most 64 MiB of HBM per device.

v0:
```python
import math

import jax
import jax.numpy as jnp
from jax import lax
from jax.sharding import PartitionSpec as P

GRID_X = 8
BATCHES = 3


def tables(points):
    counter = jnp.arange(points, dtype=jnp.int32)
    angles = (
        2.0 * math.pi / points * (counter[:, None] * counter[None, :] % points).astype(jnp.float32)
    )
    factor = 1.0 / math.sqrt(points)
    return (
        (jnp.cos(angles) * factor).astype(jnp.bfloat16),
        (-jnp.sin(angles) * factor).astype(jnp.bfloat16),
    )


def left_apply(real_part, imag_part, left_real, left_imag):
    points = real_part.shape[0]
    stacked = jnp.concatenate([real_part, imag_part], 0)
    joined = jnp.concatenate([left_real, left_imag], -1)
    product = jnp.einsum("ij,...jk->...ik", stacked, joined, preferred_element_type=jnp.float32)
    return (
        product[..., :points, :points] - product[..., points:, points:],
        product[..., :points, points:] + product[..., points:, :points],
    )


def right_apply(real_part, imag_part, left_real, left_imag):
    points = real_part.shape[0]
    stacked = jnp.concatenate([real_part, imag_part], 1)
    joined = jnp.concatenate([left_real, left_imag], -2)
    product = jnp.einsum("...ij,jk->...ik", joined, stacked, preferred_element_type=jnp.float32)
    return (
        product[..., :points, :points] - product[..., points:, points:],
        product[..., :points, points:] + product[..., points:, :points],
    )


def over_waves(terms):
    total = terms[:, 0]
    for wave in range(1, terms.shape[1]):
        total = total + terms[:, wave]
    return total


def split_exact(values):
    high = lax.reduce_precision(values, exponent_bits=8, mantissa_bits=7)
    rest = values - high
    middle = lax.reduce_precision(rest, exponent_bits=8, mantissa_bits=7)
    low = rest - middle
    return jnp.stack([high, middle, low]).astype(jnp.bfloat16)


def pick(spec, picker_matrix, values, picker_first):
    parts = split_exact(values)
    ones = picker_matrix.astype(jnp.bfloat16)
    if picker_first:
        moved = jnp.einsum(spec, ones, parts, preferred_element_type=jnp.float32)
    else:
        moved = jnp.einsum(spec, parts, ones, preferred_element_type=jnp.float32)
    return (moved[0] + moved[1]) + moved[2]


def window_terms(cells, illumination, absorb, phases, measured, alive, cos_table, sin_table):
    absorb_col = absorb[None, :, None, None]
    phase_col = phases[None, :, None, None]
    spread = cells[:, None, :, :]
    magnitude = jnp.exp(-absorb_col * spread)
    object_real = magnitude * jnp.cos(phase_col * spread)
    object_imag = magnitude * jnp.sin(phase_col * spread)
    probe_real = illumination[None, :, 0]
    probe_imag = illumination[None, :, 1]
    wave_real = probe_real * object_real - probe_imag * object_imag
    wave_imag = probe_real * object_imag + probe_imag * object_real
    half_real, half_imag = left_apply(
        cos_table, sin_table, wave_real.astype(jnp.bfloat16), wave_imag.astype(jnp.bfloat16)
    )
    far_real, far_imag = right_apply(
        cos_table, sin_table, half_real.astype(jnp.bfloat16), half_imag.astype(jnp.bfloat16)
    )
    modulus = jnp.sqrt(far_real * far_real + far_imag * far_imag + 0.25)
    ratio = measured.astype(jnp.float32) / modulus
    fixed_real = (far_real * ratio).astype(jnp.bfloat16)
    fixed_imag = (far_imag * ratio).astype(jnp.bfloat16)
    back_real, back_imag = left_apply(cos_table, -sin_table, fixed_real, fixed_imag)
    new_real, new_imag = right_apply(
        cos_table, -sin_table, back_real.astype(jnp.bfloat16), back_imag.astype(jnp.bfloat16)
    )
    wave_real, wave_imag = lax.optimization_barrier((wave_real, wave_imag))
    slope_real = -absorb_col * wave_real - phase_col * wave_imag
    slope_imag = -absorb_col * wave_imag + phase_col * wave_real
    change_real = new_real - wave_real
    change_imag = new_imag - wave_imag
    weight_live = alive.astype(jnp.float32)[:, None, None]
    numerator = over_waves(slope_real * change_real + slope_imag * change_imag) * weight_live
    weights = over_waves(slope_real * slope_real + slope_imag * slope_imag) * weight_live
    return (numerator, weights)


def tile_max(value):
    count = lax.axis_size("tile")
    spread = jnp.broadcast_to(value, (count, 128))
    gathered = lax.all_to_all(spread, "tile", 0, 0, tiled=True)
    return jnp.max(gathered)


def from_tile(block, rows, columns):
    waves, tiles = lax.axis_size("wave"), lax.axis_size("tile")
    grid_rows = tiles // GRID_X
    half = GRID_X // 2
    pairs = []
    for target in range(tiles):
        row, col = target // GRID_X + rows, target % GRID_X + columns
        if not (0 <= row < grid_rows and 0 <= col < GRID_X):
            continue
        source = row * GRID_X + col
        crossing = (col // half) != ((target % GRID_X) // half)
        for wave in range(waves):
            giver = (waves // 2 - 1 - wave // 2) * 2 + wave % 2 if crossing else wave
            pairs.append((giver * tiles + source, wave * tiles + target))
    return lax.ppermute(block, ("wave", "tile"), pairs)


def partner(block, bit):
    return lax.ppermute(block, "wave", [(i, i ^ bit) for i in range(lax.axis_size("wave"))])


def z_sum(block):
    bit = 2
    while bit < lax.axis_size("wave"):
        block = block + partner(block, bit)
        bit *= 2
    return block


def join_halves(block, core):
    other = partner(block, 1)
    low = jnp.where(core == 0, block, other)
    high = jnp.where(core == 0, other, block)
    return jnp.concatenate([low, high], -2)


def picker(offsets, size, span):
    cells = lax.broadcasted_iota(jnp.int32, (offsets.shape[0], size, span), 1)
    spots = lax.broadcasted_iota(jnp.int32, (offsets.shape[0], size, span), 2)
    return (cells == spots + offsets[:, None, None]).astype(jnp.float32)


def shards(thickness, illumination, absorb, phases, amplitudes, positions, batch_order, live_slots):
    tile_now = thickness[0]
    tile_height, tile_width = tile_now.shape
    window = illumination.shape[-1]
    slots = live_slots.shape[2]
    cos_table, sin_table = tables(window)
    core = lax.axis_index("wave") % 2
    half = tile_height // 2
    rows = lax.dynamic_slice_in_dim(tile_now, core * half, half, axis=0)
    halo = jnp.stack([from_tile(rows, 0, 1), from_tile(rows, 1, 0), from_tile(rows, 1, 1)])
    right, below, corner = join_halves(halo, core)
    extended = jnp.concatenate(
        [jnp.concatenate([tile_now, right], 1), jnp.concatenate([below, corner], 1)], 0
    )
    for batch_index in range(BATCHES):
        chosen = batch_order[0, batch_index * slots : (batch_index + 1) * slots]
        places = positions[0][chosen]
        measured = amplitudes[0][chosen]
        alive = live_slots[0, batch_index]
        row_pick = picker(places[:, 0], tile_height + window, window)
        col_pick = picker(places[:, 1], tile_width + window, window)
        strips = pick("sij,pik->psjk", row_pick, extended, True)
        cells = pick("psjk,skl->psjl", col_pick, strips, False)
        numer_win, weight_win = window_terms(
            cells, illumination, absorb, phases, measured, alive, cos_table, sin_table
        )
        wins = jnp.stack([numer_win, weight_win], 1)
        placed_rows = pick("sij,psmjk->psmik", row_pick, wins, True)
        spread = pick("psmik,slk->pmil", col_pick, placed_rows, False)
        quadrants = jnp.stack(
            [
                spread[:, :tile_height, :tile_width],
                spread[:, :tile_height, tile_width:],
                spread[:, tile_height:, :tile_width],
                spread[:, tile_height:, tile_width:],
            ]
        )
        kept = lax.dynamic_slice_in_dim(quadrants, core * half, half, axis=2)
        given = lax.dynamic_slice_in_dim(quadrants, (1 - core) * half, half, axis=2)
        quadrants = kept + partner(given, 1)
        own = quadrants[0]
        from_left = from_tile(quadrants[1], 0, -1)
        from_above = from_tile(quadrants[2], -1, 0)
        from_corner = from_tile(quadrants[3], -1, -1)
        halves = z_sum(own + from_left + from_above + from_corner)
        maps = join_halves(halves, core)
        largest = tile_max(jnp.max(maps[1]))
        if batch_index + 1 < BATCHES:
            around = jnp.stack(
                [from_tile(halves, 0, 1), from_tile(halves, 1, 0), from_tile(halves, 1, 1)]
            )
            around = join_halves(around + 0.0 * largest, core)
            maps = jnp.concatenate(
                [
                    jnp.concatenate([maps, around[0]], 2),
                    jnp.concatenate([around[1], around[2]], 2),
                ],
                1,
            )
            extended = extended + 0.5 * maps[0] / (0.75 * maps[1] + 0.25 * largest)
            tile_now = extended[:tile_height, :tile_width]
        else:
            tile_now = tile_now + 0.5 * maps[0] / (0.75 * maps[1] + 0.25 * largest)
    return tile_now[None]


def solution(mesh):
    placed = (
        P("tile", None, None),
        P("wave", None, None, None),
        P("wave"),
        P("wave"),
        P("tile", None, "wave", None, None),
        P("tile", None, None),
        P("tile", None),
        P("tile", None, None),
    )
    return jax.shard_map(
        shards, mesh=mesh, in_specs=placed, out_specs=P("tile", None, None), check_vma=False
    )
```

profile of v0, /device:TPU:1, one launch (start us, length us, event | category | flops | bytes accessed | tf_op | source)
XLA Modules:
  0.0 377.3 jit_solution(4442892810101006806)
XLA Ops:
  10.4 2.2 collective-permute-done.2
  12.6 4.0 %collective-permute-start.3 = (f32[3,128,256]{1,2,0:T(8,128)S(1)}, f32[3,128,256]{1,2,0:T(8,128)}, u32[]{:S(2)}, u32[]{:S(2)}) collective-permute-start(f32[3,128,256]{1,2,0:T(8,128)S(1)} %pad_maximum_fusion.22), channel_id=1, source_target_pairs={{0,32},{32,0},{64,96},{96,64},{128,160},{160,128},{192,224},{224,1... | collective-permute-start | bytes 1179656 | tf_op jit(solution)/shard_map/ppermute | solution.py:132
  31.0 5.1 %fusion.272 = (bf16[2,2,256,256]{3,2,0,1:T(8,128)(2,1)S(1)}, f32[2,2,256,256]{3,2,0,1:T(8,128)S(1)}, f32[2,2,256,256]{3,2,0,1:T(8,128)S(1)}, f32[2,2,256,256]{3,2,0,1:T(8,128)S(1)}) fusion(f32[2,256,256]{2,1,0:T(8,128)S(1)} %get-tuple-element.143, f32[2]{0:T(128)S(1)} %copy-done.30, f32[2,256,256]{2,1,0:T(8,128)} %copy.188, f32[2]{0:T(128)S(1)} %neg.15, ...), kind=kLoop, calls=%fused_computation.532 | loop fusion | flops 2621440 | bytes 5242896 | tf_op jit(solution)/shard_map/convert_element_type | solution.py:83
  48.5 2.6 collective-permute-done.4
  51.3 2.5 collective-permute-start.5
  53.7 4.3 %collective-permute-start.6 = (f32[2,128,256]{1,2,0:T(8,128)S(1)}, f32[2,128,256]{1,2,0:T(8,128)S(1)}, u32[]{:S(2)}, u32[]{:S(2)}) collective-permute-start(f32[2,128,256]{1,2,0:T(8,128)S(1)} %get-tuple-element.138), channel_id=1, source_target_pairs={{0,8},{32,40},{64,72},{96,104},{128,136},{160,168},{192,200},{224,... | collective-permute-start | bytes 786440 | tf_op jit(solution)/shard_map/ppermute | solution.py:128
  58.0 4.1 %collective-permute-start.7 = (f32[2,128,256]{1,2,0:T(8,128)S(1)}, f32[2,128,256]{1,2,0:T(8,128)S(1)}, u32[]{:S(2)}, u32[]{:S(2)}) collective-permute-start(f32[2,128,256]{1,2,0:T(8,128)S(1)} %get-tuple-element.137), channel_id=1, source_target_pairs={{0,9},{32,41},{64,73},{96,105},{128,137},{160,169},{192,201},{224,... | collective-permute-start | bytes 786440 | tf_op jit(solution)/shard_map/ppermute | solution.py:128
  63.2 5.6 %collective-permute-done.7 = f32[2,128,256]{1,2,0:T(8,128)S(1)} collective-permute-done((f32[2,128,256]{1,2,0:T(8,128)S(1)}, f32[2,128,256]{1,2,0:T(8,128)S(1)}, u32[]{:S(2)}, u32[]{:S(2)}) %collective-permute-start.7) | collective-permute-done | bytes 262176 | tf_op jit(solution)/shard_map/ppermute | solution.py:128
  69.4 6.1 %collective-permute-done.8 = f32[2,128,256]{1,2,0:T(8,128)S(1)} collective-permute-done((f32[2,128,256]{1,2,0:T(8,128)S(1)}, f32[2,128,256]{1,2,0:T(8,128)S(1)}, u32[]{:S(2)}, u32[]{:S(2)}) %collective-permute-start.8) | collective-permute-done | bytes 262176 | tf_op jit(solution)/shard_map/ppermute | solution.py:132
  75.6 2.2 collective-permute-start.9
  77.8 11.9 %collective-permute-done.9 = f32[2,128,256]{1,2,0:T(8,128)S(1)} collective-permute-done((f32[2,128,256]{1,2,0:T(8,128)S(1)}, f32[2,128,256]{1,2,0:T(8,128)S(1)}, u32[]{:S(2)}, u32[]{:S(2)}) %collective-permute-start.9) | collective-permute-done | bytes 262176 | tf_op jit(solution)/shard_map/ppermute | solution.py:132
  97.8 43.4 %all_to_all.18 = f32[32,1,128]{2,1,0:T(1,128)} all-to-all(f32[32,1,128]{2,1,0:T(1,128)S(1)} %broadcast_in_dim.8), channel_id=1, replica_groups=mesh['wave'=8,'tile'=32] {'tile'}, dimensions={0} | all-to-all | bytes 32768 | tf_op jit(solution)/shard_map/all_to_all | solution.py:110
  145.4 2.1 collective-permute-start.14
  165.9 5.4 %fusion.270 = (bf16[2,2,256,256]{3,2,0,1:T(8,128)(2,1)S(1)}, f32[2,2,256,256]{3,2,0,1:T(8,128)S(1)}, bf16[2,2,256,256]{3,2,0,1:T(8,128)(2,1)S(1)}, f32[2,2,256,256]{3,2,0,1:T(8,128)S(1)}) fusion(f32[2,256,256]{2,1,0:T(8,128)} %copy-done.1, f32[2]{0:T(128)S(1)} %copy-done.30, f32[2,256,256]{2,1,0:T(8,128)} %copy.211, f32[2]{0:T(128)S(1)} %neg.15, ...), kind=kLoop, calls=%fused_computation.531 | loop fusion | flops 3145728 | bytes 4718608 | tf_op jit(solution)/shard_map/convert_element_type | solution.py:83
  182.6 2.6 collective-permute-done.15
  185.4 2.4 collective-permute-start.16
  187.8 2.1 collective-permute-start.17
  189.9 2.1 collective-permute-start.18
  195.1 5.6 %collective-permute-done.18 = f32[2,128,256]{1,2,0:T(8,128)S(1)} collective-permute-done((f32[2,128,256]{1,2,0:T(8,128)S(1)}, f32[2,128,256]{1,2,0:T(8,128)S(1)}, u32[]{:S(2)}, u32[]{:S(2)}) %collective-permute-start.18) | collective-permute-done | bytes 262176 | tf_op jit(solution)/shard_map/ppermute | solution.py:128
  200.9 6.5 %collective-permute-done.19 = f32[2,128,256]{1,2,0:T(8,128)S(1)} collective-permute-done((f32[2,128,256]{1,2,0:T(8,128)S(1)}, f32[2,128,256]{1,2,0:T(8,128)S(1)}, u32[]{:S(2)}, u32[]{:S(2)}) %collective-permute-start.19) | collective-permute-done | bytes 262176 | tf_op jit(solution)/shard_map/ppermute | solution.py:132
  207.5 14.7 %collective-permute-done.20 = f32[2,128,256]{1,2,0:T(8,128)S(1)} collective-permute-done((f32[2,128,256]{1,2,0:T(8,128)S(1)}, f32[2,128,256]{1,2,0:T(8,128)S(1)}, u32[]{:S(2)}, u32[]{:S(2)}) %collective-permute-start.20) | collective-permute-done | bytes 262176 | tf_op jit(solution)/shard_map/ppermute | solution.py:132
  230.4 35.5 %all_to_all.19 = f32[32,1,128]{2,1,0:T(1,128)S(1)} all-to-all(f32[32,1,128]{2,1,0:T(1,128)S(1)} %broadcast_in_dim.9), channel_id=1, replica_groups=mesh['wave'=8,'tile'=32] {'tile'}, dimensions={0} | all-to-all | bytes 32768 | tf_op jit(solution)/shard_map/all_to_all | solution.py:110
  269.4 2.3 collective-permute-start.25
  284.6 4.5 %fusion.267 = (bf16[2,2,256,256]{3,2,0,1:T(8,128)(2,1)S(1)}, f32[2,2,256,256]{3,2,0,1:T(8,128)S(1)}, bf16[2,2,256,256]{3,2,0,1:T(8,128)(2,1)S(1)}, f32[2,2,256,256]{3,2,0,1:T(8,128)S(1)}) fusion(f32[2,256,256]{2,1,0:T(8,128)S(1)} %copy-done.2, f32[2]{0:T(128)S(1)} %copy-done.31, f32[2,256,256]{2,1,0:T(8,128)S(1)} %copy.229, f32[2]{0:T(128)S(1)} %copy-done.33, ...), kind=kLoop, calls=%fused_computation.529 | loop fusion | flops 3145728 | bytes 4718608 | tf_op jit(solution)/shard_map/convert_element_type | solution.py:83
  300.4 2.6 collective-permute-done.26
  303.2 2.2 collective-permute-start.27
  305.4 2.3 collective-permute-start.28
  307.7 2.3 collective-permute-start.29
  312.9 5.6 %collective-permute-done.29 = f32[2,128,256]{1,2,0:T(8,128)S(1)} collective-permute-done((f32[2,128,256]{1,2,0:T(8,128)S(1)}, f32[2,128,256]{1,2,0:T(8,128)S(1)}, u32[]{:S(2)}, u32[]{:S(2)}) %collective-permute-start.29) | collective-permute-done | bytes 262176 | tf_op jit(solution)/shard_map/ppermute | solution.py:128
  318.7 6.5 %collective-permute-done.30 = f32[2,128,256]{1,2,0:T(8,128)S(1)} collective-permute-done((f32[2,128,256]{1,2,0:T(8,128)S(1)}, f32[2,128,256]{1,2,0:T(8,128)S(1)}, u32[]{:S(2)}, u32[]{:S(2)}) %collective-permute-start.30) | collective-permute-done | bytes 262176 | tf_op jit(solution)/shard_map/ppermute | solution.py:132
  326.8 13.2 %collective-permute-done.31 = f32[2,128,256]{1,2,0:T(8,128)S(1)} collective-permute-done((f32[2,128,256]{1,2,0:T(8,128)S(1)}, f32[2,128,256]{1,2,0:T(8,128)S(1)}, u32[]{:S(2)}, u32[]{:S(2)}) %collective-permute-start.31) | collective-permute-done | bytes 262176 | tf_op jit(solution)/shard_map/ppermute | solution.py:132
  343.1 30.5 %all_to_all.20 = f32[32,1,128]{2,1,0:T(1,128)S(1)} all-to-all(f32[32,1,128]{2,1,0:T(1,128)S(1)} %broadcast_in_dim.10), channel_id=1, replica_groups=mesh['wave'=8,'tile'=32] {'tile'}, dimensions={0} | all-to-all | bytes 32768 | tf_op jit(solution)/shard_map/all_to_all | solution.py:110
  (274 shorter events, 126.9 us)
Async XLA Ops:
  1.1 9.2 %collective-permute-start = (f32[128,256]{0,1:T(8,128)S(1)}, f32[128,256]{0,1:T(8,128)S(1)}, u32[]{:S(2)}, u32[]{:S(2)}) collective-permute-start(f32[128,256]{0,1:T(8,128)S(1)} %bitcast.365), channel_id=1, source_target_pairs={{1,0},{33,32},{65,64},{97,96},{129,128},{161,160},{193,192},{225,2... | collective-permute-start | bytes 393224 | tf_op jit(solution)/shard_map/ppermute | solution.py:128
  2.4 8.0 %collective-permute-start.1 = (f32[128,256]{0,1:T(8,128)S(1)}, f32[128,256]{0,1:T(8,128)S(1)}, u32[]{:S(2)}, u32[]{:S(2)}) collective-permute-start(f32[128,256]{0,1:T(8,128)S(1)} %bitcast.366), channel_id=1, source_target_pairs={{8,0},{40,32},{72,64},{104,96},{136,128},{168,160},{200,192},{232,... | collective-permute-start | bytes 393224 | tf_op jit(solution)/shard_map/ppermute | solution.py:128
  3.7 8.8 %collective-permute-start.2 = (f32[128,256]{0,1:T(8,128)S(1)}, f32[128,256]{0,1:T(8,128)S(1)}, u32[]{:S(2)}, u32[]{:S(2)}) collective-permute-start(f32[128,256]{0,1:T(8,128)S(1)} %bitcast.367), channel_id=1, source_target_pairs={{9,0},{41,32},{73,64},{105,96},{137,128},{169,160},{201,192},{233,... | collective-permute-start | bytes 393224 | tf_op jit(solution)/shard_map/ppermute | solution.py:128
  12.6 11.5 %collective-permute-start.3 = (f32[3,128,256]{1,2,0:T(8,128)S(1)}, f32[3,128,256]{1,2,0:T(8,128)}, u32[]{:S(2)}, u32[]{:S(2)}) collective-permute-start(f32[3,128,256]{1,2,0:T(8,128)S(1)} %pad_maximum_fusion.22), channel_id=1, source_target_pairs={{0,32},{32,0},{64,96},{96,64},{128,160},{160,128},{192,224},{224,1... | collective-permute-start | bytes 1179656 | tf_op jit(solution)/shard_map/ppermute | solution.py:132
  48.3 2.7 collective-permute-start.4
  51.3 10.9 %collective-permute-start.5 = (f32[2,128,256]{1,2,0:T(8,128)S(1)}, f32[2,128,256]{1,2,0:T(8,128)S(1)}, u32[]{:S(2)}, u32[]{:S(2)}) collective-permute-start(f32[2,128,256]{1,2,0:T(8,128)S(1)} %get-tuple-element.136), channel_id=1, source_target_pairs={{0,1},{32,33},{64,65},{96,97},{128,129},{160,161},{192,193},{224,2... | collective-permute-start | bytes 786440 | tf_op jit(solution)/shard_map/ppermute | solution.py:128
  53.7 9.5 %collective-permute-start.6 = (f32[2,128,256]{1,2,0:T(8,128)S(1)}, f32[2,128,256]{1,2,0:T(8,128)S(1)}, u32[]{:S(2)}, u32[]{:S(2)}) collective-permute-start(f32[2,128,256]{1,2,0:T(8,128)S(1)} %get-tuple-element.138), channel_id=1, source_target_pairs={{0,8},{32,40},{64,72},{96,104},{128,136},{160,168},{192,200},{224,... | collective-permute-start | bytes 786440 | tf_op jit(solution)/shard_map/ppermute | solution.py:128
  58.0 10.8 %collective-permute-start.7 = (f32[2,128,256]{1,2,0:T(8,128)S(1)}, f32[2,128,256]{1,2,0:T(8,128)S(1)}, u32[]{:S(2)}, u32[]{:S(2)}) collective-permute-start(f32[2,128,256]{1,2,0:T(8,128)S(1)} %get-tuple-element.137), channel_id=1, source_target_pairs={{0,9},{32,41},{64,73},{96,105},{128,137},{160,169},{192,201},{224,... | collective-permute-start | bytes 786440 | tf_op jit(solution)/shard_map/ppermute | solution.py:128
  68.9 6.6 %collective-permute-start.8 = (f32[2,128,256]{1,2,0:T(8,128)S(1)}, f32[2,128,256]{1,2,0:T(8,128)S(1)}, u32[]{:S(2)}, u32[]{:S(2)}) collective-permute-start(f32[2,128,256]{1,2,0:T(8,128)S(1)} %fusion.228), channel_id=1, source_target_pairs={{0,64},{32,96},{64,0},{96,32},{128,192},{160,224},{192,128},{224,1... | collective-permute-start | bytes 786440 | tf_op jit(solution)/shard_map/ppermute | solution.py:132
  75.6 14.1 %collective-permute-start.9 = (f32[2,128,256]{1,2,0:T(8,128)S(1)}, f32[2,128,256]{1,2,0:T(8,128)S(1)}, u32[]{:S(2)}, u32[]{:S(2)}) collective-permute-start(f32[2,128,256]{1,2,0:T(8,128)S(1)} %add.553), channel_id=1, source_target_pairs={{0,128},{32,160},{64,192},{96,224},{128,0},{160,32},{192,64},{224,... | collective-permute-start | bytes 786440 | tf_op jit(solution)/shard_map/ppermute | solution.py:132
  90.4 5.1 %collective-permute-start.10 = (f32[2,128,256]{1,2,0:T(8,128)}, f32[2,128,256]{1,2,0:T(8,128)S(1)}, u32[]{:S(2)}, u32[]{:S(2)}) collective-permute-start(f32[2,128,256]{1,2,0:T(8,128)} %add.554), channel_id=1, source_target_pairs={{0,32},{32,0},{64,96},{96,64},{128,160},{160,128},{192,224},{224,1... | collective-permute-start | bytes 786440 | tf_op jit(solution)/shard_map/ppermute | solution.py:132
  91.6 51.6 %collective-permute-start.11 = (f32[2,128,256]{1,2,0:T(8,128)}, f32[2,128,256]{1,2,0:T(8,128)S(1)}, u32[]{:S(2)}, u32[]{:S(2)}) collective-permute-start(f32[2,128,256]{1,2,0:T(8,128)} %add.554), channel_id=1, source_target_pairs={{1,0},{33,32},{65,64},{97,96},{129,128},{161,160},{193,192},{225,2... | collective-permute-start | bytes 786440 | tf_op jit(solution)/shard_map/ppermute | solution.py:128
  92.9 50.4 %collective-permute-start.12 = (f32[2,128,256]{1,2,0:T(8,128)}, f32[2,128,256]{1,2,0:T(8,128)S(1)}, u32[]{:S(2)}, u32[]{:S(2)}) collective-permute-start(f32[2,128,256]{1,2,0:T(8,128)} %add.554), channel_id=1, source_target_pairs={{8,0},{40,32},{72,64},{104,96},{136,128},{168,160},{200,192},{232,... | collective-permute-start | bytes 786440 | tf_op jit(solution)/shard_map/ppermute | solution.py:128
  94.2 49.1 %collective-permute-start.13 = (f32[2,128,256]{1,2,0:T(8,128)}, f32[2,128,256]{1,2,0:T(8,128)}, u32[]{:S(2)}, u32[]{:S(2)}) collective-permute-start(f32[2,128,256]{1,2,0:T(8,128)} %add.554), channel_id=1, source_target_pairs={{9,0},{41,32},{73,64},{105,96},{137,128},{169,160},{201,192},{233,... | collective-permute-start | bytes 786440 | tf_op jit(solution)/shard_map/ppermute | solution.py:128
  145.4 9.8 %collective-permute-start.14 = (f32[3,2,128,256]{2,3,1,0:T(8,128)}, f32[3,2,128,256]{2,3,1,0:T(8,128)}, u32[]{:S(2)}, u32[]{:S(2)}) collective-permute-start(f32[3,2,128,256]{2,3,1,0:T(8,128)} %maximum_add_fusion), channel_id=1, source_target_pairs={{0,32},{32,0},{64,96},{96,64},{128,160},{160,128},{192,224},{224,1... | collective-permute-start | bytes 2359304 | tf_op jit(solution)/shard_map/ppermute | solution.py:132
  182.3 3.0 collective-permute-start.15
  185.4 7.8 %collective-permute-start.16 = (f32[2,128,256]{1,2,0:T(8,128)S(1)}, f32[2,128,256]{1,2,0:T(8,128)S(1)}, u32[]{:S(2)}, u32[]{:S(2)}) collective-permute-start(f32[2,128,256]{1,2,0:T(8,128)S(1)} %get-tuple-element.126), channel_id=1, source_target_pairs={{0,1},{32,33},{64,65},{96,97},{128,129},{160,161},{192,193},{224,2... | collective-permute-start | bytes 786440 | tf_op jit(solution)/shard_map/ppermute | solution.py:128
  187.8 7.3 %collective-permute-start.17 = (f32[2,128,256]{1,2,0:T(8,128)S(1)}, f32[2,128,256]{1,2,0:T(8,128)S(1)}, u32[]{:S(2)}, u32[]{:S(2)}) collective-permute-start(f32[2,128,256]{1,2,0:T(8,128)S(1)} %get-tuple-element.128), channel_id=1, source_target_pairs={{0,8},{32,40},{64,72},{96,104},{128,136},{160,168},{192,200},{224,... | collective-permute-start | bytes 786440 | tf_op jit(solution)/shard_map/ppermute | solution.py:128
  189.9 10.8 %collective-permute-start.18 = (f32[2,128,256]{1,2,0:T(8,128)S(1)}, f32[2,128,256]{1,2,0:T(8,128)S(1)}, u32[]{:S(2)}, u32[]{:S(2)}) collective-permute-start(f32[2,128,256]{1,2,0:T(8,128)S(1)} %get-tuple-element.127), channel_id=1, source_target_pairs={{0,9},{32,41},{64,73},{96,105},{128,137},{160,169},{192,201},{224,... | collective-permute-start | bytes 786440 | tf_op jit(solution)/shard_map/ppermute | solution.py:128
  200.8 6.6 %collective-permute-start.19 = (f32[2,128,256]{1,2,0:T(8,128)S(1)}, f32[2,128,256]{1,2,0:T(8,128)S(1)}, u32[]{:S(2)}, u32[]{:S(2)}) collective-permute-start(f32[2,128,256]{1,2,0:T(8,128)S(1)} %fusion.224), channel_id=1, source_target_pairs={{0,64},{32,96},{64,0},{96,32},{128,192},{160,224},{192,128},{224,1... | collective-permute-start | bytes 786440 | tf_op jit(solution)/shard_map/ppermute | solution.py:132
  207.4 14.8 %collective-permute-start.20 = (f32[2,128,256]{1,2,0:T(8,128)S(1)}, f32[2,128,256]{1,2,0:T(8,128)S(1)}, u32[]{:S(2)}, u32[]{:S(2)}) collective-permute-start(f32[2,128,256]{1,2,0:T(8,128)S(1)} %add.594), channel_id=1, source_target_pairs={{0,128},{32,160},{64,192},{96,224},{128,0},{160,32},{192,64},{224,... | collective-permute-start | bytes 786440 | tf_op jit(solution)/shard_map/ppermute | solution.py:132
  223.0 4.4 %collective-permute-start.21 = (f32[2,128,256]{1,2,0:T(8,128)}, f32[2,128,256]{1,2,0:T(8,128)S(1)}, u32[]{:S(2)}, u32[]{:S(2)}) collective-permute-start(f32[2,128,256]{1,2,0:T(8,128)} %add.595), channel_id=1, source_target_pairs={{0,32},{32,0},{64,96},{96,64},{128,160},{160,128},{192,224},{224,1... | collective-permute-start | bytes 786440 | tf_op jit(solution)/shard_map/ppermute | solution.py:132
  223.5 43.8 %collective-permute-start.22 = (f32[2,128,256]{1,2,0:T(8,128)}, f32[2,128,256]{1,2,0:T(8,128)}, u32[]{:S(2)}, u32[]{:S(2)}) collective-permute-start(f32[2,128,256]{1,2,0:T(8,128)} %add.595), channel_id=1, source_target_pairs={{1,0},{33,32},{65,64},{97,96},{129,128},{161,160},{193,192},{225,2... | collective-permute-start | bytes 786440 | tf_op jit(solution)/shard_map/ppermute | solution.py:128
  224.8 42.5 %collective-permute-start.23 = (f32[2,128,256]{1,2,0:T(8,128)}, f32[2,128,256]{1,2,0:T(8,128)}, u32[]{:S(2)}, u32[]{:S(2)}) collective-permute-start(f32[2,128,256]{1,2,0:T(8,128)} %add.595), channel_id=1, source_target_pairs={{8,0},{40,32},{72,64},{104,96},{136,128},{168,160},{200,192},{232,... | collective-permute-start | bytes 786440 | tf_op jit(solution)/shard_map/ppermute | solution.py:128
  226.1 41.2 %collective-permute-start.24 = (f32[2,128,256]{1,2,0:T(8,128)}, f32[2,128,256]{1,2,0:T(8,128)}, u32[]{:S(2)}, u32[]{:S(2)}) collective-permute-start(f32[2,128,256]{1,2,0:T(8,128)} %add.595), channel_id=1, source_target_pairs={{9,0},{41,32},{73,64},{105,96},{137,128},{169,160},{201,192},{233,... | collective-permute-start | bytes 786440 | tf_op jit(solution)/shard_map/ppermute | solution.py:128
  269.4 6.5 %collective-permute-start.25 = (f32[3,2,128,256]{2,3,1,0:T(8,128)}, f32[3,2,128,256]{2,3,1,0:T(8,128)}, u32[]{:S(2)}, u32[]{:S(2)}) collective-permute-start(f32[3,2,128,256]{2,3,1,0:T(8,128)} %maximum_add_fusion.1), channel_id=1, source_target_pairs={{0,32},{32,0},{64,96},{96,64},{128,160},{160,128},{192,224},{224,1... | collective-permute-start | bytes 2359304 | tf_op jit(solution)/shard_map/ppermute | solution.py:132
  300.0 3.0 collective-permute-start.26
  303.2 7.7 %collective-permute-start.27 = (f32[2,128,256]{1,2,0:T(8,128)S(1)}, f32[2,128,256]{1,2,0:T(8,128)S(1)}, u32[]{:S(2)}, u32[]{:S(2)}) collective-permute-start(f32[2,128,256]{1,2,0:T(8,128)S(1)} %get-tuple-element.118), channel_id=1, source_target_pairs={{0,1},{32,33},{64,65},{96,97},{128,129},{160,161},{192,193},{224,2... | collective-permute-start | bytes 786440 | tf_op jit(solution)/shard_map/ppermute | solution.py:128
  305.4 7.4 %collective-permute-start.28 = (f32[2,128,256]{1,2,0:T(8,128)S(1)}, f32[2,128,256]{1,2,0:T(8,128)S(1)}, u32[]{:S(2)}, u32[]{:S(2)}) collective-permute-start(f32[2,128,256]{1,2,0:T(8,128)S(1)} %get-tuple-element.120), channel_id=1, source_target_pairs={{0,8},{32,40},{64,72},{96,104},{128,136},{160,168},{192,200},{224,... | collective-permute-start | bytes 786440 | tf_op jit(solution)/shard_map/ppermute | solution.py:128
  307.7 10.8 %collective-permute-start.29 = (f32[2,128,256]{1,2,0:T(8,128)S(1)}, f32[2,128,256]{1,2,0:T(8,128)S(1)}, u32[]{:S(2)}, u32[]{:S(2)}) collective-permute-start(f32[2,128,256]{1,2,0:T(8,128)S(1)} %get-tuple-element.119), channel_id=1, source_target_pairs={{0,9},{32,41},{64,73},{96,105},{128,137},{160,169},{192,201},{224,... | collective-permute-start | bytes 786440 | tf_op jit(solution)/shard_map/ppermute | solution.py:128
  318.6 6.6 %collective-permute-start.30 = (f32[2,128,256]{1,2,0:T(8,128)S(1)}, f32[2,128,256]{1,2,0:T(8,128)S(1)}, u32[]{:S(2)}, u32[]{:S(2)}) collective-permute-start(f32[2,128,256]{1,2,0:T(8,128)S(1)} %fusion.219), channel_id=1, source_target_pairs={{0,64},{32,96},{64,0},{96,32},{128,192},{160,224},{192,128},{224,1... | collective-permute-start | bytes 786440 | tf_op jit(solution)/shard_map/ppermute | solution.py:132
  325.2 14.8 %collective-permute-start.31 = (f32[2,128,256]{1,2,0:T(8,128)S(1)}, f32[2,128,256]{1,2,0:T(8,128)S(1)}, u32[]{:S(2)}, u32[]{:S(2)}) collective-permute-start(f32[2,128,256]{1,2,0:T(8,128)S(1)} %add.635), channel_id=1, source_target_pairs={{0,128},{32,160},{64,192},{96,224},{128,0},{160,32},{192,64},{224,... | collective-permute-start | bytes 786440 | tf_op jit(solution)/shard_map/ppermute | solution.py:132
  (45 other events, 578.9 us)
where the time goes:
time: 382 us; the launch traced here: 377 us
  blocking collectives  110 us (29%)
  waiting for transfers between devices  94.2 us (25%)
  other arithmetic  61.1 us (16%)
  starting transfers between devices  51.9 us (14%)
  local copies, waits for them, and re-layouts  32.1 us (8%)
  matrix products  23.4 us (6%)
  between operations  5.13 us (1%)
    all_to_all x3, blocking collectives, tile_max(): gathered = lax.all_to_all(spread, 'tile', 0, 0, tiled=True)  110 us
    ppermute x15, waiting for transfers between devices, partner(): lax.ppermute(block, 'wave', [(i, i ^ bit) for i in range(lax.axis_size('w...  68.2 us
    ppermute x18, starting transfers between devices, from_tile(): return lax.ppermute(block, ('wave', 'tile'), pairs)  35.8 us
    ppermute x18, waiting for transfers between devices, from_tile(): return lax.ppermute(block, ('wave', 'tile'), pairs)  26 us
    ppermute x15, starting transfers between devices, partner(): lax.ppermute(block, 'wave', [(i, i ^ bit) for i in range(lax.axis_size('w...  16.1 us
    convert_element_type x3, other arithmetic, window_terms(): wave_imag.astype(jnp.bfloat16)  10.1 us
    unnamed x89, local copies, waits for them, and re-layouts  9.27 us
    another operation x20, other arithmetic  8.74 us
  transfers between devices with their start and end apart: 33, of which 19 were waited for; matrix products, arithmetic and copies ran while one was open for 8% of the time, Pallas kernels for 0%

commit v1 on v0

--- a/solution.py
+++ b/solution.py
@@ -201,19 +201,17 @@
         maps = join_halves(halves, core)
         largest = tile_max(jnp.max(maps[1]))
         if batch_index + 1 < BATCHES:
-            around = jnp.stack(
-                [from_tile(halves, 0, 1), from_tile(halves, 1, 0), from_tile(halves, 1, 1)]
+            around = jnp.stack([from_tile(halves, 0, 1), from_tile(halves, 1, 0)])
+            around = join_halves(around + 0.0 * largest, core)
+            maps = jnp.concatenate([jnp.stack([maps, around[0]]), around[1][None]])
+            near = jnp.stack([tile_now, extended[:tile_height, tile_width:], extended[tile_height:, :tile_width]])
+            near = near + 0.5 * maps[:, 0] / (0.75 * maps[:, 1] + 0.25 * largest)
+            tile_now = near[0]
+            rows = lax.dynamic_slice_in_dim(tile_now, core * half, half, axis=0)
+            corner = join_halves(from_tile(rows, 1, 1), core)
+            extended = jnp.concatenate(
+                [jnp.concatenate([near[0], near[1]], 1), jnp.concatenate([near[2], corner], 1)], 0
             )
-            around = join_halves(around + 0.0 * largest, core)
-            maps = jnp.concatenate(
-                [
-                    jnp.concatenate([maps, around[0]], 2),
-                    jnp.concatenate([around[1], around[2]], 2),
-                ],
-                1,
-            )
-            extended = extended + 0.5 * maps[0] / (0.75 * maps[1] + 0.25 * largest)
-            tile_now = extended[:tile_height, :tile_width]
         else:
             tile_now = tile_now + 0.5 * maps[0] / (0.75 * maps[1] + 0.25 * largest)
     return tile_now[None]

time: 382 us -> 406 us (1.063)
  waiting for transfers between devices: 94.2 us -> 106 us
  other arithmetic: 61.1 us -> 67.6 us
    ppermute x18, waiting for transfers between devices: 26 us -> 35.7 us  [from_tile(): return lax.ppermute(block, ('wave', 'tile'), pairs)]
    ppermute x15 -> x17, waiting for transfers between devices: 68.2 us -> 70 us  [partner(): lax.ppermute(block, 'wave', [(i, i ^ bit) for i in range(lax.axis_size('w...]
    ppermute x15 -> x17, starting transfers between devices: 16.1 us -> 16.3 us  [partner(): lax.ppermute(block, 'wave', [(i, i ^ bit) for i in range(lax.axis_size('w...]
    unnamed x89 -> x77, local copies, waits for them, and re-layouts: 9.27 us -> 9.2 us
  transfers between devices with their start and end apart: 33 -> 35, of which waited for: 19 -> 22; matrix products, arithmetic and copies ran while one was open for 8% -> 9% of each run, Pallas kernels for 0% -> 0%
where the time goes in v1:
time: 406 us; the launch traced here: 401 us
  blocking collectives  112 us (28%)
  waiting for transfers between devices  106 us (26%)
  other arithmetic  67.6 us (17%)
  starting transfers between devices  51.9 us (13%)
  local copies, waits for them, and re-layouts  35.7 us (9%)
  matrix products  23.4 us (6%)
  between operations  5.14 us (1%)
    all_to_all x3, blocking collectives, tile_max(): gathered = lax.all_to_all(spread, 'tile', 0, 0, tiled=True)  112 us
    ppermute x17, waiting for transfers between devices, partner(): lax.ppermute(block, 'wave', [(i, i ^ bit) for i in range(lax.axis_size('w...  70 us
    ppermute x18, waiting for transfers between devices, from_tile(): return lax.ppermute(block, ('wave', 'tile'), pairs)  35.7 us
    ppermute x18, starting transfers between devices, from_tile(): return lax.ppermute(block, ('wave', 'tile'), pairs)  35.6 us
    ppermute x17, starting transfers between devices, partner(): lax.ppermute(block, 'wave', [(i, i ^ bit) for i in range(lax.axis_size('w...  16.3 us
    convert_element_type x3, other arithmetic, window_terms(): wave_imag.astype(jnp.bfloat16)  9.94 us
    unnamed x77, local copies, waits for them, and re-layouts  9.2 us
  transfers between devices with their start and end apart: 35, of which 22 were waited for; matrix products, arithmetic and copies ran while one was open for 9% of the time, Pallas kernels for 0%

profile of v1, /device:TPU:1, one launch (start us, length us, event | category | flops | bytes accessed | tf_op | source)
XLA Modules:
  0.0 401.5 jit_solution(8950373188910977440)
XLA Ops:
  10.3 2.2 collective-permute-done.2
  13.4 3.9 collective-permute-start.3
  33.1 5.1 %fusion.264 = (bf16[2,2,256,256]{3,2,0,1:T(8,128)(2,1)S(1)}, f32[2,2,256,256]{3,2,0,1:T(8,128)S(1)}, f32[2,2,256,256]{3,2,0,1:T(8,128)S(1)}, f32[2,2,256,256]{3,2,0,1:T(8,128)S(1)}) fusion(f32[2,256,256]{2,1,0:T(8,128)S(1)} %get-tuple-element.134, f32[2]{0:T(128)S(1)} %copy-done.26, f32[2,256,256]{2,1,0:T(8,128)} %copy.192, f32[2]{0:T(128)S(1)} %neg.15, ...), kind=kLoop, calls=%fused_computation.536 | loop fusion | flops 2621440 | bytes 5242896 | tf_op jit(solution)/shard_map/convert_element_type | solution.py:83
  50.3 2.6 collective-permute-done.4
  53.2 2.5 collective-permute-start.5
  55.6 4.3 %collective-permute-start.6 = (f32[2,128,256]{1,2,0:T(8,128)S(1)}, f32[2,128,256]{1,2,0:T(8,128)S(1)}, u32[]{:S(2)}, u32[]{:S(2)}) collective-permute-start(f32[2,128,256]{1,2,0:T(8,128)S(1)} %get-tuple-element.129), channel_id=1, source_target_pairs={{0,8},{32,40},{64,72},{96,104},{128,136},{160,168},{192,200},{224,... | collective-permute-start | bytes 786440 | tf_op jit(solution)/shard_map/ppermute | solution.py:128
  59.9 4.1 %collective-permute-start.7 = (f32[2,128,256]{1,2,0:T(8,128)S(1)}, f32[2,128,256]{1,2,0:T(8,128)S(1)}, u32[]{:S(2)}, u32[]{:S(2)}) collective-permute-start(f32[2,128,256]{1,2,0:T(8,128)S(1)} %get-tuple-element.128), channel_id=1, source_target_pairs={{0,9},{32,41},{64,73},{96,105},{128,137},{160,169},{192,201},{224,... | collective-permute-start | bytes 786440 | tf_op jit(solution)/shard_map/ppermute | solution.py:128
  65.1 5.6 %collective-permute-done.7 = f32[2,128,256]{1,2,0:T(8,128)S(1)} collective-permute-done((f32[2,128,256]{1,2,0:T(8,128)S(1)}, f32[2,128,256]{1,2,0:T(8,128)S(1)}, u32[]{:S(2)}, u32[]{:S(2)}) %collective-permute-start.7) | collective-permute-done | bytes 262176 | tf_op jit(solution)/shard_map/ppermute | solution.py:128
  71.3 6.1 %collective-permute-done.8 = f32[2,128,256]{1,2,0:T(8,128)S(1)} collective-permute-done((f32[2,128,256]{1,2,0:T(8,128)S(1)}, f32[2,128,256]{1,2,0:T(8,128)S(1)}, u32[]{:S(2)}, u32[]{:S(2)}) %collective-permute-start.8) | collective-permute-done | bytes 262176 | tf_op jit(solution)/shard_map/ppermute | solution.py:132
  77.5 2.2 collective-permute-start.9
  79.7 11.9 %collective-permute-done.9 = f32[2,128,256]{1,2,0:T(8,128)S(1)} collective-permute-done((f32[2,128,256]{1,2,0:T(8,128)S(1)}, f32[2,128,256]{1,2,0:T(8,128)S(1)}, u32[]{:S(2)}, u32[]{:S(2)}) %collective-permute-start.9) | collective-permute-done | bytes 262176 | tf_op jit(solution)/shard_map/ppermute | solution.py:132
  99.2 41.1 %all_to_all.18 = f32[32,1,128]{2,1,0:T(1,128)} all-to-all(f32[32,1,128]{2,1,0:T(1,128)S(1)} %broadcast_in_dim.6), channel_id=1, replica_groups=mesh['wave'=8,'tile'=32] {'tile'}, dimensions={0} | all-to-all | bytes 32768 | tf_op jit(solution)/shard_map/all_to_all | solution.py:110
  144.3 2.2 collective-permute-start.13
  157.5 2.7 collective-permute-done.14
  175.4 5.3 %fusion.263 = (bf16[2,2,256,256]{3,2,0,1:T(8,128)(2,1)S(1)}, f32[2,2,256,256]{3,2,0,1:T(8,128)S(1)}, bf16[2,2,256,256]{3,2,0,1:T(8,128)(2,1)S(1)}, f32[2,2,256,256]{3,2,0,1:T(8,128)S(1)}) fusion(f32[2,256,256]{2,1,0:T(8,128)S(1)} %get-tuple-element.134, f32[2]{0:T(128)S(1)} %copy-done.26, f32[2,256,256]{2,1,0:T(8,128)} %copy.215, f32[2]{0:T(128)S(1)} %neg.15, ...), kind=kLoop, calls=%fused_computation.535 | loop fusion | flops 3145728 | bytes 4718608 | tf_op jit(solution)/shard_map/convert_element_type | solution.py:83
  192.4 2.6 collective-permute-done.16
  197.3 2.4 collective-permute-start.18
  202.8 2.1 collective-permute-done.18
  204.9 5.6 %collective-permute-done.19 = f32[2,128,256]{1,2,0:T(8,128)S(1)} collective-permute-done((f32[2,128,256]{1,2,0:T(8,128)S(1)}, f32[2,128,256]{1,2,0:T(8,128)S(1)}, u32[]{:S(2)}, u32[]{:S(2)}) %collective-permute-start.19) | collective-permute-done | bytes 262176 | tf_op jit(solution)/shard_map/ppermute | solution.py:128
  210.7 6.5 %collective-permute-done.20 = f32[2,128,256]{1,2,0:T(8,128)S(1)} collective-permute-done((f32[2,128,256]{1,2,0:T(8,128)S(1)}, f32[2,128,256]{1,2,0:T(8,128)S(1)}, u32[]{:S(2)}, u32[]{:S(2)}) %collective-permute-start.20) | collective-permute-done | bytes 262176 | tf_op jit(solution)/shard_map/ppermute | solution.py:132
  217.4 14.7 %collective-permute-done.21 = f32[2,128,256]{1,2,0:T(8,128)S(1)} collective-permute-done((f32[2,128,256]{1,2,0:T(8,128)S(1)}, f32[2,128,256]{1,2,0:T(8,128)S(1)}, u32[]{:S(2)}, u32[]{:S(2)}) %collective-permute-start.21) | collective-permute-done | bytes 262176 | tf_op jit(solution)/shard_map/ppermute | solution.py:132
  239.0 37.2 %all_to_all.19 = f32[32,1,128]{2,1,0:T(1,128)S(1)} all-to-all(f32[32,1,128]{2,1,0:T(1,128)S(1)} %broadcast_in_dim.7), channel_id=1, replica_groups=mesh['wave'=8,'tile'=32] {'tile'}, dimensions={0} | all-to-all | bytes 32768 | tf_op jit(solution)/shard_map/all_to_all | solution.py:110
  288.7 6.7 %collective-permute-done.26 = f32[128,256]{0,1:T(8,128)} collective-permute-done((f32[128,256]{0,1:T(8,128)S(1)}, f32[128,256]{0,1:T(8,128)}, u32[]{:S(2)}, u32[]{:S(2)}) %collective-permute-start.26) | collective-permute-done | bytes 131104 | tf_op jit(solution)/shard_map/ppermute | solution.py:128
  305.2 4.5 %fusion.261 = (bf16[2,2,256,256]{3,2,0,1:T(8,128)(2,1)S(1)}, f32[2,2,256,256]{3,2,0,1:T(8,128)S(1)}, bf16[2,2,256,256]{3,2,0,1:T(8,128)(2,1)S(1)}, f32[2,2,256,256]{3,2,0,1:T(8,128)S(1)}) fusion(f32[2,256,256]{2,1,0:T(8,128)S(1)} %get-tuple-element.134, f32[2]{0:T(128)S(1)} %copy-done.27, f32[2,256,256]{2,1,0:T(8,128)S(1)} %copy.233, f32[2]{0:T(128)S(1)} %copy-done.29, ...), kind=kLoop, calls=%fused_computation.533 | loop fusion | flops 3145728 | bytes 4718608 | tf_op jit(solution)/shard_map/convert_element_type | solution.py:83
  321.4 2.6 collective-permute-done.28
  324.2 2.2 collective-permute-start.29
  326.5 2.3 collective-permute-start.30
  328.7 2.1 collective-permute-start.31
  333.9 5.6 %collective-permute-done.31 = f32[2,128,256]{1,2,0:T(8,128)S(1)} collective-permute-done((f32[2,128,256]{1,2,0:T(8,128)S(1)}, f32[2,128,256]{1,2,0:T(8,128)S(1)}, u32[]{:S(2)}, u32[]{:S(2)}) %collective-permute-start.31) | collective-permute-done | bytes 262176 | tf_op jit(solution)/shard_map/ppermute | solution.py:128
  339.7 6.5 %collective-permute-done.32 = f32[2,128,256]{1,2,0:T(8,128)S(1)} collective-permute-done((f32[2,128,256]{1,2,0:T(8,128)S(1)}, f32[2,128,256]{1,2,0:T(8,128)S(1)}, u32[]{:S(2)}, u32[]{:S(2)}) %collective-permute-start.32) | collective-permute-done | bytes 262176 | tf_op jit(solution)/shard_map/ppermute | solution.py:132
  346.4 14.7 %collective-permute-done.33 = f32[2,128,256]{1,2,0:T(8,128)S(1)} collective-permute-done((f32[2,128,256]{1,2,0:T(8,128)S(1)}, f32[2,128,256]{1,2,0:T(8,128)S(1)}, u32[]{:S(2)}, u32[]{:S(2)}) %collective-permute-start.33) | collective-permute-done | bytes 262176 | tf_op jit(solution)/shard_map/ppermute | solution.py:132
  364.2 33.6 %all_to_all.20 = f32[32,1,128]{2,1,0:T(1,128)S(1)} all-to-all(f32[32,1,128]{2,1,0:T(1,128)S(1)} %broadcast_in_dim.8), channel_id=1, replica_groups=mesh['wave'=8,'tile'=32] {'tile'}, dimensions={0} | all-to-all | bytes 32768 | tf_op jit(solution)/shard_map/all_to_all | solution.py:110
  (277 shorter events, 142.2 us)
Async XLA Ops:
  1.1 9.2 %collective-permute-start = (f32[128,256]{0,1:T(8,128)S(1)}, f32[128,256]{0,1:T(8,128)S(1)}, u32[]{:S(2)}, u32[]{:S(2)}) collective-permute-start(f32[128,256]{0,1:T(8,128)S(1)} %bitcast.370), channel_id=1, source_target_pairs={{1,0},{33,32},{65,64},{97,96},{129,128},{161,160},{193,192},{225,2... | collective-permute-start | bytes 393224 | tf_op jit(solution)/shard_map/ppermute | solution.py:128
  2.4 7.9 %collective-permute-start.1 = (f32[128,256]{0,1:T(8,128)S(1)}, f32[128,256]{0,1:T(8,128)S(1)}, u32[]{:S(2)}, u32[]{:S(2)}) collective-permute-start(f32[128,256]{0,1:T(8,128)S(1)} %bitcast.371), channel_id=1, source_target_pairs={{8,0},{40,32},{72,64},{104,96},{136,128},{168,160},{200,192},{232,... | collective-permute-start | bytes 393224 | tf_op jit(solution)/shard_map/ppermute | solution.py:128
  3.7 8.8 %collective-permute-start.2 = (f32[128,256]{0,1:T(8,128)S(1)}, f32[128,256]{0,1:T(8,128)S(1)}, u32[]{:S(2)}, u32[]{:S(2)}) collective-permute-start(f32[128,256]{0,1:T(8,128)S(1)} %bitcast.372), channel_id=1, source_target_pairs={{9,0},{41,32},{73,64},{105,96},{137,128},{169,160},{201,192},{233,... | collective-permute-start | bytes 393224 | tf_op jit(solution)/shard_map/ppermute | solution.py:128
  13.4 11.5 %collective-permute-start.3 = (f32[3,128,256]{1,2,0:T(8,128)}, f32[3,128,256]{1,2,0:T(8,128)}, u32[]{:S(2)}, u32[]{:S(2)}) collective-permute-start(f32[3,128,256]{1,2,0:T(8,128)} %pad_maximum_fusion.24), channel_id=1, source_target_pairs={{0,32},{32,0},{64,96},{96,64},{128,160},{160,128},{192,224},{224,1... | collective-permute-start | bytes 1179656 | tf_op jit(solution)/shard_map/ppermute | solution.py:132
  53.2 10.8 %collective-permute-start.5 = (f32[2,128,256]{1,2,0:T(8,128)S(1)}, f32[2,128,256]{1,2,0:T(8,128)S(1)}, u32[]{:S(2)}, u32[]{:S(2)}) collective-permute-start(f32[2,128,256]{1,2,0:T(8,128)S(1)} %get-tuple-element.127), channel_id=1, source_target_pairs={{0,1},{32,33},{64,65},{96,97},{128,129},{160,161},{192,193},{224,2... | collective-permute-start | bytes 786440 | tf_op jit(solution)/shard_map/ppermute | solution.py:128
  55.6 9.5 %collective-permute-start.6 = (f32[2,128,256]{1,2,0:T(8,128)S(1)}, f32[2,128,256]{1,2,0:T(8,128)S(1)}, u32[]{:S(2)}, u32[]{:S(2)}) collective-permute-start(f32[2,128,256]{1,2,0:T(8,128)S(1)} %get-tuple-element.129), channel_id=1, source_target_pairs={{0,8},{32,40},{64,72},{96,104},{128,136},{160,168},{192,200},{224,... | collective-permute-start | bytes 786440 | tf_op jit(solution)/shard_map/ppermute | solution.py:128
  59.9 10.8 %collective-permute-start.7 = (f32[2,128,256]{1,2,0:T(8,128)S(1)}, f32[2,128,256]{1,2,0:T(8,128)S(1)}, u32[]{:S(2)}, u32[]{:S(2)}) collective-permute-start(f32[2,128,256]{1,2,0:T(8,128)S(1)} %get-tuple-element.128), channel_id=1, source_target_pairs={{0,9},{32,41},{64,73},{96,105},{128,137},{160,169},{192,201},{224,... | collective-permute-start | bytes 786440 | tf_op jit(solution)/shard_map/ppermute | solution.py:128
  70.8 6.6 %collective-permute-start.8 = (f32[2,128,256]{1,2,0:T(8,128)S(1)}, f32[2,128,256]{1,2,0:T(8,128)S(1)}, u32[]{:S(2)}, u32[]{:S(2)}) collective-permute-start(f32[2,128,256]{1,2,0:T(8,128)S(1)} %fusion.223), channel_id=1, source_target_pairs={{0,64},{32,96},{64,0},{96,32},{128,192},{160,224},{192,128},{224,1... | collective-permute-start | bytes 786440 | tf_op jit(solution)/shard_map/ppermute | solution.py:132
  77.5 14.1 %collective-permute-start.9 = (f32[2,128,256]{1,2,0:T(8,128)S(1)}, f32[2,128,256]{1,2,0:T(8,128)S(1)}, u32[]{:S(2)}, u32[]{:S(2)}) collective-permute-start(f32[2,128,256]{1,2,0:T(8,128)S(1)} %add.534), channel_id=1, source_target_pairs={{0,128},{32,160},{64,192},{96,224},{128,0},{160,32},{192,64},{224,... | collective-permute-start | bytes 786440 | tf_op jit(solution)/shard_map/ppermute | solution.py:132
  92.3 3.8 collective-permute-start.10
  93.5 48.8 %collective-permute-start.11 = (f32[2,128,256]{1,2,0:T(8,128)}, f32[2,128,256]{1,2,0:T(8,128)}, u32[]{:S(2)}, u32[]{:S(2)}) collective-permute-start(f32[2,128,256]{1,2,0:T(8,128)} %add.535), channel_id=1, source_target_pairs={{1,0},{33,32},{65,64},{97,96},{129,128},{161,160},{193,192},{225,2... | collective-permute-start | bytes 786440 | tf_op jit(solution)/shard_map/ppermute | solution.py:128
  94.8 47.6 %collective-permute-start.12 = (f32[2,128,256]{1,2,0:T(8,128)}, f32[2,128,256]{1,2,0:T(8,128)}, u32[]{:S(2)}, u32[]{:S(2)}) collective-permute-start(f32[2,128,256]{1,2,0:T(8,128)} %add.535), channel_id=1, source_target_pairs={{8,0},{40,32},{72,64},{104,96},{136,128},{168,160},{200,192},{232,... | collective-permute-start | bytes 786440 | tf_op jit(solution)/shard_map/ppermute | solution.py:128
  144.3 4.0 %collective-permute-start.13 = (f32[2,2,128,256]{2,3,1,0:T(8,128)}, f32[2,2,128,256]{2,3,1,0:T(8,128)}, u32[]{:S(2)}, u32[]{:S(2)}) collective-permute-start(f32[2,2,128,256]{2,3,1,0:T(8,128)} %maximum_add_fusion), channel_id=1, source_target_pairs={{0,32},{32,0},{64,96},{96,64},{128,160},{160,128},{192,224},{224,1... | collective-permute-start | bytes 1572872 | tf_op jit(solution)/shard_map/ppermute | solution.py:132
  152.4 7.8 %collective-permute-start.14 = (f32[128,256]{0,1:T(8,128)}, f32[128,256]{0,1:T(8,128)}, u32[]{:S(2)}, u32[]{:S(2)}) collective-permute-start(f32[128,256]{0,1:T(8,128)} %dynamic-slice_bitcast_fusion.1), channel_id=1, source_target_pairs={{9,0},{41,32},{73,64},{105,96},{137,128},{169,160},{201,192},{233,... | collective-permute-start | bytes 393224 | tf_op jit(solution)/shard_map/ppermute | solution.py:128
  160.2 7.4 %collective-permute-start.15 = (f32[128,256]{0,1:T(8,128)}, f32[128,256]{0,1:T(8,128)}, u32[]{:S(2)}, u32[]{:S(2)}) collective-permute-start(f32[128,256]{0,1:T(8,128)} %collective-permute-done.14), channel_id=1, source_target_pairs={{0,32},{32,0},{64,96},{96,64},{128,160},{160,128},{192,224},{224,1... | collective-permute-start | bytes 393224 | tf_op jit(solution)/shard_map/ppermute | solution.py:132
  195.2 7.5 %collective-permute-start.17 = (f32[2,128,256]{1,2,0:T(8,128)S(1)}, f32[2,128,256]{1,2,0:T(8,128)S(1)}, u32[]{:S(2)}, u32[]{:S(2)}) collective-permute-start(f32[2,128,256]{1,2,0:T(8,128)S(1)} %get-tuple-element.114), channel_id=1, source_target_pairs={{0,1},{32,33},{64,65},{96,97},{128,129},{160,161},{192,193},{224,2... | collective-permute-start | bytes 786440 | tf_op jit(solution)/shard_map/ppermute | solution.py:128
  197.3 7.6 %collective-permute-start.18 = (f32[2,128,256]{1,2,0:T(8,128)S(1)}, f32[2,128,256]{1,2,0:T(8,128)S(1)}, u32[]{:S(2)}, u32[]{:S(2)}) collective-permute-start(f32[2,128,256]{1,2,0:T(8,128)S(1)} %get-tuple-element.116), channel_id=1, source_target_pairs={{0,8},{32,40},{64,72},{96,104},{128,136},{160,168},{192,200},{224,... | collective-permute-start | bytes 786440 | tf_op jit(solution)/shard_map/ppermute | solution.py:128
  199.7 10.8 %collective-permute-start.19 = (f32[2,128,256]{1,2,0:T(8,128)S(1)}, f32[2,128,256]{1,2,0:T(8,128)S(1)}, u32[]{:S(2)}, u32[]{:S(2)}) collective-permute-start(f32[2,128,256]{1,2,0:T(8,128)S(1)} %get-tuple-element.115), channel_id=1, source_target_pairs={{0,9},{32,41},{64,73},{96,105},{128,137},{160,169},{192,201},{224,... | collective-permute-start | bytes 786440 | tf_op jit(solution)/shard_map/ppermute | solution.py:128
  210.6 6.6 %collective-permute-start.20 = (f32[2,128,256]{1,2,0:T(8,128)S(1)}, f32[2,128,256]{1,2,0:T(8,128)S(1)}, u32[]{:S(2)}, u32[]{:S(2)}) collective-permute-start(f32[2,128,256]{1,2,0:T(8,128)S(1)} %fusion.220), channel_id=1, source_target_pairs={{0,64},{32,96},{64,0},{96,32},{128,192},{160,224},{192,128},{224,1... | collective-permute-start | bytes 786440 | tf_op jit(solution)/shard_map/ppermute | solution.py:132
  217.3 14.8 %collective-permute-start.21 = (f32[2,128,256]{1,2,0:T(8,128)S(1)}, f32[2,128,256]{1,2,0:T(8,128)S(1)}, u32[]{:S(2)}, u32[]{:S(2)}) collective-permute-start(f32[2,128,256]{1,2,0:T(8,128)S(1)} %add.574), channel_id=1, source_target_pairs={{0,128},{32,160},{64,192},{96,224},{128,0},{160,32},{192,64},{224,... | collective-permute-start | bytes 786440 | tf_op jit(solution)/shard_map/ppermute | solution.py:132
  232.8 3.1 collective-permute-start.22
  233.3 44.2 %collective-permute-start.24 = (f32[2,128,256]{1,2,0:T(8,128)}, f32[2,128,256]{1,2,0:T(8,128)}, u32[]{:S(2)}, u32[]{:S(2)}) collective-permute-start(f32[2,128,256]{1,2,0:T(8,128)} %add.575), channel_id=1, source_target_pairs={{8,0},{40,32},{72,64},{104,96},{136,128},{168,160},{200,192},{232,... | collective-permute-start | bytes 786440 | tf_op jit(solution)/shard_map/ppermute | solution.py:128
  234.6 43.0 %collective-permute-start.23 = (f32[2,128,256]{1,2,0:T(8,128)}, f32[2,128,256]{1,2,0:T(8,128)}, u32[]{:S(2)}, u32[]{:S(2)}) collective-permute-start(f32[2,128,256]{1,2,0:T(8,128)} %add.575), channel_id=1, source_target_pairs={{1,0},{33,32},{65,64},{97,96},{129,128},{161,160},{193,192},{225,2... | collective-permute-start | bytes 786440 | tf_op jit(solution)/shard_map/ppermute | solution.py:128
  279.4 4.6 %collective-permute-start.25 = (f32[2,2,128,256]{2,3,1,0:T(8,128)}, f32[2,2,128,256]{2,3,1,0:T(8,128)}, u32[]{:S(2)}, u32[]{:S(2)}) collective-permute-start(f32[2,2,128,256]{2,3,1,0:T(8,128)} %maximum_add_fusion.1), channel_id=1, source_target_pairs={{0,32},{32,0},{64,96},{96,64},{128,160},{160,128},{192,224},{224,1... | collective-permute-start | bytes 1572872 | tf_op jit(solution)/shard_map/ppermute | solution.py:132
  287.4 8.0 %collective-permute-start.26 = (f32[128,256]{0,1:T(8,128)S(1)}, f32[128,256]{0,1:T(8,128)}, u32[]{:S(2)}, u32[]{:S(2)}) collective-permute-start(f32[128,256]{0,1:T(8,128)S(1)} %dynamic-slice_bitcast_fusion), channel_id=1, source_target_pairs={{9,0},{41,32},{73,64},{105,96},{137,128},{169,160},{201,192},{233,... | collective-permute-start | bytes 393224 | tf_op jit(solution)/shard_map/ppermute | solution.py:128
  295.4 3.7 collective-permute-start.27
  321.0 3.0 collective-permute-start.28
  324.2 7.7 %collective-permute-start.29 = (f32[2,128,256]{1,2,0:T(8,128)S(1)}, f32[2,128,256]{1,2,0:T(8,128)S(1)}, u32[]{:S(2)}, u32[]{:S(2)}) collective-permute-start(f32[2,128,256]{1,2,0:T(8,128)S(1)} %get-tuple-element.101), channel_id=1, source_target_pairs={{0,1},{32,33},{64,65},{96,97},{128,129},{160,161},{192,193},{224,2... | collective-permute-start | bytes 786440 | tf_op jit(solution)/shard_map/ppermute | solution.py:128
  326.5 7.4 %collective-permute-start.30 = (f32[2,128,256]{1,2,0:T(8,128)S(1)}, f32[2,128,256]{1,2,0:T(8,128)S(1)}, u32[]{:S(2)}, u32[]{:S(2)}) collective-permute-start(f32[2,128,256]{1,2,0:T(8,128)S(1)} %get-tuple-element.103), channel_id=1, source_target_pairs={{0,8},{32,40},{64,72},{96,104},{128,136},{160,168},{192,200},{224,... | collective-permute-start | bytes 786440 | tf_op jit(solution)/shard_map/ppermute | solution.py:128
  328.7 10.8 %collective-permute-start.31 = (f32[2,128,256]{1,2,0:T(8,128)S(1)}, f32[2,128,256]{1,2,0:T(8,128)S(1)}, u32[]{:S(2)}, u32[]{:S(2)}) collective-permute-start(f32[2,128,256]{1,2,0:T(8,128)S(1)} %get-tuple-element.102), channel_id=1, source_target_pairs={{0,9},{32,41},{64,73},{96,105},{128,137},{160,169},{192,201},{224,... | collective-permute-start | bytes 786440 | tf_op jit(solution)/shard_map/ppermute | solution.py:128
  339.6 6.6 %collective-permute-start.32 = (f32[2,128,256]{1,2,0:T(8,128)S(1)}, f32[2,128,256]{1,2,0:T(8,128)S(1)}, u32[]{:S(2)}, u32[]{:S(2)}) collective-permute-start(f32[2,128,256]{1,2,0:T(8,128)S(1)} %fusion.217), channel_id=1, source_target_pairs={{0,64},{32,96},{64,0},{96,32},{128,192},{160,224},{192,128},{224,1... | collective-permute-start | bytes 786440 | tf_op jit(solution)/shard_map/ppermute | solution.py:132
  346.3 14.8 %collective-permute-start.33 = (f32[2,128,256]{1,2,0:T(8,128)S(1)}, f32[2,128,256]{1,2,0:T(8,128)S(1)}, u32[]{:S(2)}, u32[]{:S(2)}) collective-permute-start(f32[2,128,256]{1,2,0:T(8,128)S(1)} %add.614), channel_id=1, source_target_pairs={{0,128},{32,160},{64,192},{96,224},{128,0},{160,32},{192,64},{224,... | collective-permute-start | bytes 786440 | tf_op jit(solution)/shard_map/ppermute | solution.py:132
  (41 other events, 394.2 us)

commit v2 on v0

--- a/solution.py
+++ b/solution.py
@@ -123,7 +123,7 @@
         source = row * GRID_X + col
         crossing = (col // half) != ((target % GRID_X) // half)
         for wave in range(waves):
-            giver = (waves // 2 - 1 - wave // 2) * 2 + wave % 2 if crossing else wave
+            giver = ((wave // 2 + 2) % (waves // 2)) * 2 + wave % 2 if crossing else wave
             pairs.append((giver * tiles + source, wave * tiles + target))
     return lax.ppermute(block, ("wave", "tile"), pairs)
 

time: 382 us -> 379 us (level)
  no operation moved by 1% of the time
where the time goes in v2:
time: 379 us; the launch traced here: 374 us
  blocking collectives  107 us (28%)
  waiting for transfers between devices  94.2 us (25%)
  other arithmetic  61.1 us (16%)
  starting transfers between devices  51.6 us (14%)
  local copies, waits for them, and re-layouts  32.1 us (8%)
  matrix products  23.4 us (6%)
  between operations  5.14 us (1%)
    all_to_all x3, blocking collectives, tile_max(): gathered = lax.all_to_all(spread, 'tile', 0, 0, tiled=True)  107 us
    ppermute x15, waiting for transfers between devices, partner(): lax.ppermute(block, 'wave', [(i, i ^ bit) for i in range(lax.axis_size('w...  68.2 us
    ppermute x18, starting transfers between devices, from_tile(): return lax.ppermute(block, ('wave', 'tile'), pairs)  35.8 us
    ppermute x18, waiting for transfers between devices, from_tile(): return lax.ppermute(block, ('wave', 'tile'), pairs)  26 us
    ppermute x15, starting transfers between devices, partner(): lax.ppermute(block, 'wave', [(i, i ^ bit) for i in range(lax.axis_size('w...  15.8 us
    convert_element_type x3, other arithmetic, window_terms(): wave_imag.astype(jnp.bfloat16)  10.1 us
    unnamed x89, local copies, waits for them, and re-layouts  9.27 us
    another operation x20, other arithmetic  8.74 us
  transfers between devices with their start and end apart: 33, of which 19 were waited for; matrix products, arithmetic and copies ran while one was open for 8% of the time, Pallas kernels for 0%

profile of v2, /device:TPU:1, one launch (start us, length us, event | category | flops | bytes accessed | tf_op | source)
XLA Modules:
  0.0 374.3 jit_solution(2119289986798747667)
XLA Ops:
  10.4 2.2 collective-permute-done.2
  12.6 4.0 %collective-permute-start.3 = (f32[3,128,256]{1,2,0:T(8,128)S(1)}, f32[3,128,256]{1,2,0:T(8,128)}, u32[]{:S(2)}, u32[]{:S(2)}) collective-permute-start(f32[3,128,256]{1,2,0:T(8,128)S(1)} %pad_maximum_fusion.22), channel_id=1, source_target_pairs={{0,32},{32,0},{64,96},{96,64},{128,160},{160,128},{192,224},{224,1... | collective-permute-start | bytes 1179656 | tf_op jit(solution)/shard_map/ppermute | solution.py:132
  31.0 5.1 %fusion.272 = (bf16[2,2,256,256]{3,2,0,1:T(8,128)(2,1)S(1)}, f32[2,2,256,256]{3,2,0,1:T(8,128)S(1)}, f32[2,2,256,256]{3,2,0,1:T(8,128)S(1)}, f32[2,2,256,256]{3,2,0,1:T(8,128)S(1)}) fusion(f32[2,256,256]{2,1,0:T(8,128)S(1)} %get-tuple-element.143, f32[2]{0:T(128)S(1)} %copy-done.30, f32[2,256,256]{2,1,0:T(8,128)} %copy.188, f32[2]{0:T(128)S(1)} %neg.15, ...), kind=kLoop, calls=%fused_computation.532 | loop fusion | flops 2621440 | bytes 5242896 | tf_op jit(solution)/shard_map/convert_element_type | solution.py:83
  48.5 2.6 collective-permute-done.4
  51.3 2.5 collective-permute-start.5
  53.7 4.3 %collective-permute-start.6 = (f32[2,128,256]{1,2,0:T(8,128)S(1)}, f32[2,128,256]{1,2,0:T(8,128)S(1)}, u32[]{:S(2)}, u32[]{:S(2)}) collective-permute-start(f32[2,128,256]{1,2,0:T(8,128)S(1)} %get-tuple-element.138), channel_id=1, source_target_pairs={{0,8},{32,40},{64,72},{96,104},{128,136},{160,168},{192,200},{224,... | collective-permute-start | bytes 786440 | tf_op jit(solution)/shard_map/ppermute | solution.py:128
  58.0 4.1 %collective-permute-start.7 = (f32[2,128,256]{1,2,0:T(8,128)S(1)}, f32[2,128,256]{1,2,0:T(8,128)S(1)}, u32[]{:S(2)}, u32[]{:S(2)}) collective-permute-start(f32[2,128,256]{1,2,0:T(8,128)S(1)} %get-tuple-element.137), channel_id=1, source_target_pairs={{0,9},{32,41},{64,73},{96,105},{128,137},{160,169},{192,201},{224,... | collective-permute-start | bytes 786440 | tf_op jit(solution)/shard_map/ppermute | solution.py:128
  63.2 5.6 %collective-permute-done.7 = f32[2,128,256]{1,2,0:T(8,128)S(1)} collective-permute-done((f32[2,128,256]{1,2,0:T(8,128)S(1)}, f32[2,128,256]{1,2,0:T(8,128)S(1)}, u32[]{:S(2)}, u32[]{:S(2)}) %collective-permute-start.7) | collective-permute-done | bytes 262176 | tf_op jit(solution)/shard_map/ppermute | solution.py:128
  69.4 6.1 %collective-permute-done.8 = f32[2,128,256]{1,2,0:T(8,128)S(1)} collective-permute-done((f32[2,128,256]{1,2,0:T(8,128)S(1)}, f32[2,128,256]{1,2,0:T(8,128)S(1)}, u32[]{:S(2)}, u32[]{:S(2)}) %collective-permute-start.8) | collective-permute-done | bytes 262176 | tf_op jit(solution)/shard_map/ppermute | solution.py:132
  75.6 2.2 collective-permute-start.9
  77.8 11.9 %collective-permute-done.9 = f32[2,128,256]{1,2,0:T(8,128)S(1)} collective-permute-done((f32[2,128,256]{1,2,0:T(8,128)S(1)}, f32[2,128,256]{1,2,0:T(8,128)S(1)}, u32[]{:S(2)}, u32[]{:S(2)}) %collective-permute-start.9) | collective-permute-done | bytes 262176 | tf_op jit(solution)/shard_map/ppermute | solution.py:132
  97.8 41.7 %all_to_all.18 = f32[32,1,128]{2,1,0:T(1,128)} all-to-all(f32[32,1,128]{2,1,0:T(1,128)S(1)} %broadcast_in_dim.8), channel_id=1, replica_groups=mesh['wave'=8,'tile'=32] {'tile'}, dimensions={0} | all-to-all | bytes 32768 | tf_op jit(solution)/shard_map/all_to_all | solution.py:110
  163.9 5.4 %fusion.270 = (bf16[2,2,256,256]{3,2,0,1:T(8,128)(2,1)S(1)}, f32[2,2,256,256]{3,2,0,1:T(8,128)S(1)}, bf16[2,2,256,256]{3,2,0,1:T(8,128)(2,1)S(1)}, f32[2,2,256,256]{3,2,0,1:T(8,128)S(1)}) fusion(f32[2,256,256]{2,1,0:T(8,128)} %copy-done.1, f32[2]{0:T(128)S(1)} %copy-done.30, f32[2,256,256]{2,1,0:T(8,128)} %copy.211, f32[2]{0:T(128)S(1)} %neg.15, ...), kind=kLoop, calls=%fused_computation.531 | loop fusion | flops 3145728 | bytes 4718608 | tf_op jit(solution)/shard_map/convert_element_type | solution.py:83
  180.6 2.6 collective-permute-done.15
  183.4 2.4 collective-permute-start.16
  185.8 2.1 collective-permute-start.17
  187.9 2.1 collective-permute-start.18
  193.1 5.6 %collective-permute-done.18 = f32[2,128,256]{1,2,0:T(8,128)S(1)} collective-permute-done((f32[2,128,256]{1,2,0:T(8,128)S(1)}, f32[2,128,256]{1,2,0:T(8,128)S(1)}, u32[]{:S(2)}, u32[]{:S(2)}) %collective-permute-start.18) | collective-permute-done | bytes 262176 | tf_op jit(solution)/shard_map/ppermute | solution.py:128
  198.9 6.5 %collective-permute-done.19 = f32[2,128,256]{1,2,0:T(8,128)S(1)} collective-permute-done((f32[2,128,256]{1,2,0:T(8,128)S(1)}, f32[2,128,256]{1,2,0:T(8,128)S(1)}, u32[]{:S(2)}, u32[]{:S(2)}) %collective-permute-start.19) | collective-permute-done | bytes 262176 | tf_op jit(solution)/shard_map/ppermute | solution.py:132
  205.6 14.7 %collective-permute-done.20 = f32[2,128,256]{1,2,0:T(8,128)S(1)} collective-permute-done((f32[2,128,256]{1,2,0:T(8,128)S(1)}, f32[2,128,256]{1,2,0:T(8,128)S(1)}, u32[]{:S(2)}, u32[]{:S(2)}) %collective-permute-start.20) | collective-permute-done | bytes 262176 | tf_op jit(solution)/shard_map/ppermute | solution.py:132
  228.4 35.1 %all_to_all.19 = f32[32,1,128]{2,1,0:T(1,128)S(1)} all-to-all(f32[32,1,128]{2,1,0:T(1,128)S(1)} %broadcast_in_dim.9), channel_id=1, replica_groups=mesh['wave'=8,'tile'=32] {'tile'}, dimensions={0} | all-to-all | bytes 32768 | tf_op jit(solution)/shard_map/all_to_all | solution.py:110
  264.9 2.1 maximum_add_fusion.1
  267.0 2.3 collective-permute-start.25
  282.2 4.5 %fusion.267 = (bf16[2,2,256,256]{3,2,0,1:T(8,128)(2,1)S(1)}, f32[2,2,256,256]{3,2,0,1:T(8,128)S(1)}, bf16[2,2,256,256]{3,2,0,1:T(8,128)(2,1)S(1)}, f32[2,2,256,256]{3,2,0,1:T(8,128)S(1)}) fusion(f32[2,256,256]{2,1,0:T(8,128)S(1)} %copy-done.2, f32[2]{0:T(128)S(1)} %copy-done.31, f32[2,256,256]{2,1,0:T(8,128)S(1)} %copy.229, f32[2]{0:T(128)S(1)} %copy-done.33, ...), kind=kLoop, calls=%fused_computation.529 | loop fusion | flops 3145728 | bytes 4718608 | tf_op jit(solution)/shard_map/convert_element_type | solution.py:83
  298.0 2.6 collective-permute-done.26
  300.8 2.2 collective-permute-start.27
  303.1 2.3 collective-permute-start.28
  305.4 2.2 collective-permute-start.29
  310.5 5.6 %collective-permute-done.29 = f32[2,128,256]{1,2,0:T(8,128)S(1)} collective-permute-done((f32[2,128,256]{1,2,0:T(8,128)S(1)}, f32[2,128,256]{1,2,0:T(8,128)S(1)}, u32[]{:S(2)}, u32[]{:S(2)}) %collective-permute-start.29) | collective-permute-done | bytes 262176 | tf_op jit(solution)/shard_map/ppermute | solution.py:128
  316.3 6.5 %collective-permute-done.30 = f32[2,128,256]{1,2,0:T(8,128)S(1)} collective-permute-done((f32[2,128,256]{1,2,0:T(8,128)S(1)}, f32[2,128,256]{1,2,0:T(8,128)S(1)}, u32[]{:S(2)}, u32[]{:S(2)}) %collective-permute-start.30) | collective-permute-done | bytes 262176 | tf_op jit(solution)/shard_map/ppermute | solution.py:132
  324.4 13.3 %collective-permute-done.31 = f32[2,128,256]{1,2,0:T(8,128)S(1)} collective-permute-done((f32[2,128,256]{1,2,0:T(8,128)S(1)}, f32[2,128,256]{1,2,0:T(8,128)S(1)}, u32[]{:S(2)}, u32[]{:S(2)}) %collective-permute-start.31) | collective-permute-done | bytes 262176 | tf_op jit(solution)/shard_map/ppermute | solution.py:132
  340.7 29.9 %all_to_all.20 = f32[32,1,128]{2,1,0:T(1,128)S(1)} all-to-all(f32[32,1,128]{2,1,0:T(1,128)S(1)} %broadcast_in_dim.10), channel_id=1, replica_groups=mesh['wave'=8,'tile'=32] {'tile'}, dimensions={0} | all-to-all | bytes 32768 | tf_op jit(solution)/shard_map/all_to_all | solution.py:110
  (274 shorter events, 126.6 us)
Async XLA Ops:
  1.1 9.2 %collective-permute-start = (f32[128,256]{0,1:T(8,128)S(1)}, f32[128,256]{0,1:T(8,128)S(1)}, u32[]{:S(2)}, u32[]{:S(2)}) collective-permute-start(f32[128,256]{0,1:T(8,128)S(1)} %bitcast.365), channel_id=1, source_target_pairs={{1,0},{33,32},{65,64},{97,96},{129,128},{161,160},{193,192},{225,2... | collective-permute-start | bytes 393224 | tf_op jit(solution)/shard_map/ppermute | solution.py:128
  2.4 8.0 %collective-permute-start.1 = (f32[128,256]{0,1:T(8,128)S(1)}, f32[128,256]{0,1:T(8,128)S(1)}, u32[]{:S(2)}, u32[]{:S(2)}) collective-permute-start(f32[128,256]{0,1:T(8,128)S(1)} %bitcast.366), channel_id=1, source_target_pairs={{8,0},{40,32},{72,64},{104,96},{136,128},{168,160},{200,192},{232,... | collective-permute-start | bytes 393224 | tf_op jit(solution)/shard_map/ppermute | solution.py:128
  3.7 8.8 %collective-permute-start.2 = (f32[128,256]{0,1:T(8,128)S(1)}, f32[128,256]{0,1:T(8,128)S(1)}, u32[]{:S(2)}, u32[]{:S(2)}) collective-permute-start(f32[128,256]{0,1:T(8,128)S(1)} %bitcast.367), channel_id=1, source_target_pairs={{9,0},{41,32},{73,64},{105,96},{137,128},{169,160},{201,192},{233,... | collective-permute-start | bytes 393224 | tf_op jit(solution)/shard_map/ppermute | solution.py:128
  12.6 11.5 %collective-permute-start.3 = (f32[3,128,256]{1,2,0:T(8,128)S(1)}, f32[3,128,256]{1,2,0:T(8,128)}, u32[]{:S(2)}, u32[]{:S(2)}) collective-permute-start(f32[3,128,256]{1,2,0:T(8,128)S(1)} %pad_maximum_fusion.22), channel_id=1, source_target_pairs={{0,32},{32,0},{64,96},{96,64},{128,160},{160,128},{192,224},{224,1... | collective-permute-start | bytes 1179656 | tf_op jit(solution)/shard_map/ppermute | solution.py:132
  48.3 2.7 collective-permute-start.4
  51.3 10.9 %collective-permute-start.5 = (f32[2,128,256]{1,2,0:T(8,128)S(1)}, f32[2,128,256]{1,2,0:T(8,128)S(1)}, u32[]{:S(2)}, u32[]{:S(2)}) collective-permute-start(f32[2,128,256]{1,2,0:T(8,128)S(1)} %get-tuple-element.136), channel_id=1, source_target_pairs={{0,1},{32,33},{64,65},{96,97},{128,129},{160,161},{192,193},{224,2... | collective-permute-start | bytes 786440 | tf_op jit(solution)/shard_map/ppermute | solution.py:128
  53.7 9.5 %collective-permute-start.6 = (f32[2,128,256]{1,2,0:T(8,128)S(1)}, f32[2,128,256]{1,2,0:T(8,128)S(1)}, u32[]{:S(2)}, u32[]{:S(2)}) collective-permute-start(f32[2,128,256]{1,2,0:T(8,128)S(1)} %get-tuple-element.138), channel_id=1, source_target_pairs={{0,8},{32,40},{64,72},{96,104},{128,136},{160,168},{192,200},{224,... | collective-permute-start | bytes 786440 | tf_op jit(solution)/shard_map/ppermute | solution.py:128
  58.0 10.8 %collective-permute-start.7 = (f32[2,128,256]{1,2,0:T(8,128)S(1)}, f32[2,128,256]{1,2,0:T(8,128)S(1)}, u32[]{:S(2)}, u32[]{:S(2)}) collective-permute-start(f32[2,128,256]{1,2,0:T(8,128)S(1)} %get-tuple-element.137), channel_id=1, source_target_pairs={{0,9},{32,41},{64,73},{96,105},{128,137},{160,169},{192,201},{224,... | collective-permute-start | bytes 786440 | tf_op jit(solution)/shard_map/ppermute | solution.py:128
  68.9 6.6 %collective-permute-start.8 = (f32[2,128,256]{1,2,0:T(8,128)S(1)}, f32[2,128,256]{1,2,0:T(8,128)S(1)}, u32[]{:S(2)}, u32[]{:S(2)}) collective-permute-start(f32[2,128,256]{1,2,0:T(8,128)S(1)} %fusion.228), channel_id=1, source_target_pairs={{0,64},{32,96},{64,0},{96,32},{128,192},{160,224},{192,128},{224,1... | collective-permute-start | bytes 786440 | tf_op jit(solution)/shard_map/ppermute | solution.py:132
  75.6 14.1 %collective-permute-start.9 = (f32[2,128,256]{1,2,0:T(8,128)S(1)}, f32[2,128,256]{1,2,0:T(8,128)S(1)}, u32[]{:S(2)}, u32[]{:S(2)}) collective-permute-start(f32[2,128,256]{1,2,0:T(8,128)S(1)} %add.553), channel_id=1, source_target_pairs={{0,128},{32,160},{64,192},{96,224},{128,0},{160,32},{192,64},{224,... | collective-permute-start | bytes 786440 | tf_op jit(solution)/shard_map/ppermute | solution.py:132
  90.4 5.1 %collective-permute-start.10 = (f32[2,128,256]{1,2,0:T(8,128)}, f32[2,128,256]{1,2,0:T(8,128)S(1)}, u32[]{:S(2)}, u32[]{:S(2)}) collective-permute-start(f32[2,128,256]{1,2,0:T(8,128)} %add.554), channel_id=1, source_target_pairs={{0,32},{32,0},{64,96},{96,64},{128,160},{160,128},{192,224},{224,1... | collective-permute-start | bytes 786440 | tf_op jit(solution)/shard_map/ppermute | solution.py:132
  91.6 49.9 %collective-permute-start.11 = (f32[2,128,256]{1,2,0:T(8,128)}, f32[2,128,256]{1,2,0:T(8,128)S(1)}, u32[]{:S(2)}, u32[]{:S(2)}) collective-permute-start(f32[2,128,256]{1,2,0:T(8,128)} %add.554), channel_id=1, source_target_pairs={{1,0},{33,32},{65,64},{97,96},{129,128},{161,160},{193,192},{225,2... | collective-permute-start | bytes 786440 | tf_op jit(solution)/shard_map/ppermute | solution.py:128
  92.9 48.7 %collective-permute-start.12 = (f32[2,128,256]{1,2,0:T(8,128)}, f32[2,128,256]{1,2,0:T(8,128)S(1)}, u32[]{:S(2)}, u32[]{:S(2)}) collective-permute-start(f32[2,128,256]{1,2,0:T(8,128)} %add.554), channel_id=1, source_target_pairs={{8,0},{40,32},{72,64},{104,96},{136,128},{168,160},{200,192},{232,... | collective-permute-start | bytes 786440 | tf_op jit(solution)/shard_map/ppermute | solution.py:128
  94.2 47.4 %collective-permute-start.13 = (f32[2,128,256]{1,2,0:T(8,128)}, f32[2,128,256]{1,2,0:T(8,128)}, u32[]{:S(2)}, u32[]{:S(2)}) collective-permute-start(f32[2,128,256]{1,2,0:T(8,128)} %add.554), channel_id=1, source_target_pairs={{9,0},{41,32},{73,64},{105,96},{137,128},{169,160},{201,192},{233,... | collective-permute-start | bytes 786440 | tf_op jit(solution)/shard_map/ppermute | solution.py:128
  143.7 9.5 %collective-permute-start.14 = (f32[3,2,128,256]{2,3,1,0:T(8,128)}, f32[3,2,128,256]{2,3,1,0:T(8,128)}, u32[]{:S(2)}, u32[]{:S(2)}) collective-permute-start(f32[3,2,128,256]{2,3,1,0:T(8,128)} %maximum_add_fusion), channel_id=1, source_target_pairs={{0,32},{32,0},{64,96},{96,64},{128,160},{160,128},{192,224},{224,1... | collective-permute-start | bytes 2359304 | tf_op jit(solution)/shard_map/ppermute | solution.py:132
  180.3 3.0 collective-permute-start.15
  183.4 7.8 %collective-permute-start.16 = (f32[2,128,256]{1,2,0:T(8,128)S(1)}, f32[2,128,256]{1,2,0:T(8,128)S(1)}, u32[]{:S(2)}, u32[]{:S(2)}) collective-permute-start(f32[2,128,256]{1,2,0:T(8,128)S(1)} %get-tuple-element.126), channel_id=1, source_target_pairs={{0,1},{32,33},{64,65},{96,97},{128,129},{160,161},{192,193},{224,2... | collective-permute-start | bytes 786440 | tf_op jit(solution)/shard_map/ppermute | solution.py:128
  185.8 7.3 %collective-permute-start.17 = (f32[2,128,256]{1,2,0:T(8,128)S(1)}, f32[2,128,256]{1,2,0:T(8,128)S(1)}, u32[]{:S(2)}, u32[]{:S(2)}) collective-permute-start(f32[2,128,256]{1,2,0:T(8,128)S(1)} %get-tuple-element.128), channel_id=1, source_target_pairs={{0,8},{32,40},{64,72},{96,104},{128,136},{160,168},{192,200},{224,... | collective-permute-start | bytes 786440 | tf_op jit(solution)/shard_map/ppermute | solution.py:128
  187.9 10.8 %collective-permute-start.18 = (f32[2,128,256]{1,2,0:T(8,128)S(1)}, f32[2,128,256]{1,2,0:T(8,128)S(1)}, u32[]{:S(2)}, u32[]{:S(2)}) collective-permute-start(f32[2,128,256]{1,2,0:T(8,128)S(1)} %get-tuple-element.127), channel_id=1, source_target_pairs={{0,9},{32,41},{64,73},{96,105},{128,137},{160,169},{192,201},{224,... | collective-permute-start | bytes 786440 | tf_op jit(solution)/shard_map/ppermute | solution.py:128
  198.8 6.6 %collective-permute-start.19 = (f32[2,128,256]{1,2,0:T(8,128)S(1)}, f32[2,128,256]{1,2,0:T(8,128)S(1)}, u32[]{:S(2)}, u32[]{:S(2)}) collective-permute-start(f32[2,128,256]{1,2,0:T(8,128)S(1)} %fusion.224), channel_id=1, source_target_pairs={{0,64},{32,96},{64,0},{96,32},{128,192},{160,224},{192,128},{224,1... | collective-permute-start | bytes 786440 | tf_op jit(solution)/shard_map/ppermute | solution.py:132
  205.5 14.8 %collective-permute-start.20 = (f32[2,128,256]{1,2,0:T(8,128)S(1)}, f32[2,128,256]{1,2,0:T(8,128)S(1)}, u32[]{:S(2)}, u32[]{:S(2)}) collective-permute-start(f32[2,128,256]{1,2,0:T(8,128)S(1)} %add.594), channel_id=1, source_target_pairs={{0,128},{32,160},{64,192},{96,224},{128,0},{160,32},{192,64},{224,... | collective-permute-start | bytes 786440 | tf_op jit(solution)/shard_map/ppermute | solution.py:132
  221.0 4.4 %collective-permute-start.21 = (f32[2,128,256]{1,2,0:T(8,128)}, f32[2,128,256]{1,2,0:T(8,128)S(1)}, u32[]{:S(2)}, u32[]{:S(2)}) collective-permute-start(f32[2,128,256]{1,2,0:T(8,128)} %add.595), channel_id=1, source_target_pairs={{0,32},{32,0},{64,96},{96,64},{128,160},{160,128},{192,224},{224,1... | collective-permute-start | bytes 786440 | tf_op jit(solution)/shard_map/ppermute | solution.py:132
  221.5 43.4 %collective-permute-start.22 = (f32[2,128,256]{1,2,0:T(8,128)}, f32[2,128,256]{1,2,0:T(8,128)}, u32[]{:S(2)}, u32[]{:S(2)}) collective-permute-start(f32[2,128,256]{1,2,0:T(8,128)} %add.595), channel_id=1, source_target_pairs={{1,0},{33,32},{65,64},{97,96},{129,128},{161,160},{193,192},{225,2... | collective-permute-start | bytes 786440 | tf_op jit(solution)/shard_map/ppermute | solution.py:128
  222.8 42.1 %collective-permute-start.23 = (f32[2,128,256]{1,2,0:T(8,128)}, f32[2,128,256]{1,2,0:T(8,128)}, u32[]{:S(2)}, u32[]{:S(2)}) collective-permute-start(f32[2,128,256]{1,2,0:T(8,128)} %add.595), channel_id=1, source_target_pairs={{8,0},{40,32},{72,64},{104,96},{136,128},{168,160},{200,192},{232,... | collective-permute-start | bytes 786440 | tf_op jit(solution)/shard_map/ppermute | solution.py:128
  224.1 40.8 %collective-permute-start.24 = (f32[2,128,256]{1,2,0:T(8,128)}, f32[2,128,256]{1,2,0:T(8,128)}, u32[]{:S(2)}, u32[]{:S(2)}) collective-permute-start(f32[2,128,256]{1,2,0:T(8,128)} %add.595), channel_id=1, source_target_pairs={{9,0},{41,32},{73,64},{105,96},{137,128},{169,160},{201,192},{233,... | collective-permute-start | bytes 786440 | tf_op jit(solution)/shard_map/ppermute | solution.py:128
  267.0 6.5 %collective-permute-start.25 = (f32[3,2,128,256]{2,3,1,0:T(8,128)}, f32[3,2,128,256]{2,3,1,0:T(8,128)}, u32[]{:S(2)}, u32[]{:S(2)}) collective-permute-start(f32[3,2,128,256]{2,3,1,0:T(8,128)} %maximum_add_fusion.1), channel_id=1, source_target_pairs={{0,32},{32,0},{64,96},{96,64},{128,160},{160,128},{192,224},{224,1... | collective-permute-start | bytes 2359304 | tf_op jit(solution)/shard_map/ppermute | solution.py:132
  297.6 3.0 collective-permute-start.26
  300.8 7.7 %collective-permute-start.27 = (f32[2,128,256]{1,2,0:T(8,128)S(1)}, f32[2,128,256]{1,2,0:T(8,128)S(1)}, u32[]{:S(2)}, u32[]{:S(2)}) collective-permute-start(f32[2,128,256]{1,2,0:T(8,128)S(1)} %get-tuple-element.118), channel_id=1, source_target_pairs={{0,1},{32,33},{64,65},{96,97},{128,129},{160,161},{192,193},{224,2... | collective-permute-start | bytes 786440 | tf_op jit(solution)/shard_map/ppermute | solution.py:128
  303.1 7.4 %collective-permute-start.28 = (f32[2,128,256]{1,2,0:T(8,128)S(1)}, f32[2,128,256]{1,2,0:T(8,128)S(1)}, u32[]{:S(2)}, u32[]{:S(2)}) collective-permute-start(f32[2,128,256]{1,2,0:T(8,128)S(1)} %get-tuple-element.120), channel_id=1, source_target_pairs={{0,8},{32,40},{64,72},{96,104},{128,136},{160,168},{192,200},{224,... | collective-permute-start | bytes 786440 | tf_op jit(solution)/shard_map/ppermute | solution.py:128
  305.4 10.8 %collective-permute-start.29 = (f32[2,128,256]{1,2,0:T(8,128)S(1)}, f32[2,128,256]{1,2,0:T(8,128)S(1)}, u32[]{:S(2)}, u32[]{:S(2)}) collective-permute-start(f32[2,128,256]{1,2,0:T(8,128)S(1)} %get-tuple-element.119), channel_id=1, source_target_pairs={{0,9},{32,41},{64,73},{96,105},{128,137},{160,169},{192,201},{224,... | collective-permute-start | bytes 786440 | tf_op jit(solution)/shard_map/ppermute | solution.py:128
  316.2 6.6 %collective-permute-start.30 = (f32[2,128,256]{1,2,0:T(8,128)S(1)}, f32[2,128,256]{1,2,0:T(8,128)S(1)}, u32[]{:S(2)}, u32[]{:S(2)}) collective-permute-start(f32[2,128,256]{1,2,0:T(8,128)S(1)} %fusion.219), channel_id=1, source_target_pairs={{0,64},{32,96},{64,0},{96,32},{128,192},{160,224},{192,128},{224,1... | collective-permute-start | bytes 786440 | tf_op jit(solution)/shard_map/ppermute | solution.py:132
  322.9 14.8 %collective-permute-start.31 = (f32[2,128,256]{1,2,0:T(8,128)S(1)}, f32[2,128,256]{1,2,0:T(8,128)S(1)}, u32[]{:S(2)}, u32[]{:S(2)}) collective-permute-start(f32[2,128,256]{1,2,0:T(8,128)S(1)} %add.635), channel_id=1, source_target_pairs={{0,128},{32,160},{64,192},{96,224},{128,0},{160,32},{192,64},{224,... | collective-permute-start | bytes 786440 | tf_op jit(solution)/shard_map/ppermute | solution.py:132
  (45 other events, 570.8 us)

commit v3 on v2

--- a/solution.py
+++ b/solution.py
@@ -141,9 +141,9 @@
 
 
 def join_halves(block, core):
-    other = partner(block, 1)
-    low = jnp.where(core == 0, block, other)
-    high = jnp.where(core == 0, other, block)
+    pair = jnp.stack([block, partner(block, 1)])
+    low = lax.dynamic_index_in_dim(pair, core, 0, keepdims=False)
+    high = lax.dynamic_index_in_dim(pair, 1 - core, 0, keepdims=False)
     return jnp.concatenate([low, high], -2)
 
 

time: 379 us -> 408 us (1.077)
  local copies, waits for them, and re-layouts: 32.1 us -> 49.6 us
  other arithmetic: 61.1 us -> 70.4 us
  blocking collectives: 107 us -> 114 us
  waiting for transfers between devices: 94.2 us -> 88.9 us
    dynamic_slice x0 -> x12, local copies, waits for them, and re-layouts: none -> 15.5 us  [the longest x6 8.6 us: join_halves(): high = lax.dynamic_index_in_dim(pair, 1 - core, 0, keepdims=False)]
    another operation x20 -> x26, other arithmetic: 8.74 us -> 17.6 us  [the longest x6 9.28 us: join_halves(): pair = jnp.stack([block, partner(block, 1)])]
    ppermute x18, waiting for transfers between devices: 26 us -> 18.6 us  [from_tile(): return lax.ppermute(block, ('wave', 'tile'), pairs)]
    all_to_all x3, blocking collectives: 107 us -> 114 us  [tile_max(): gathered = lax.all_to_all(spread, 'tile', 0, 0, tiled=True)]
    select_n x6 -> x0, other arithmetic: 6.25 us -> none  [the longest x5 6.21 us: join_halves(): low = jnp.where(core == 0, block, other)]
    unnamed x89 -> x77, local copies, waits for them, and re-layouts: 9.27 us -> 7.71 us
  transfers between devices with their start and end apart: 33 -> 33, of which waited for: 19 -> 17; matrix products, arithmetic and copies ran while one was open for 8% -> 9% of each run, Pallas kernels for 0% -> 0%
where the time goes in v3:
time: 408 us; the launch traced here: 403 us
  blocking collectives  114 us (28%)
  waiting for transfers between devices  88.9 us (22%)
  other arithmetic  70.4 us (17%)
  starting transfers between devices  51.9 us (13%)
  local copies, waits for them, and re-layouts  49.6 us (12%)
  matrix products  23.7 us (6%)
  between operations  4.53 us (1%)
    all_to_all x3, blocking collectives, tile_max(): gathered = lax.all_to_all(spread, 'tile', 0, 0, tiled=True)  114 us
    ppermute x15, waiting for transfers between devices, partner(): lax.ppermute(block, 'wave', [(i, i ^ bit) for i in range(lax.axis_size('w...  70.3 us
    ppermute x18, starting transfers between devices, from_tile(): return lax.ppermute(block, ('wave', 'tile'), pairs)  38.3 us
    ppermute x18, waiting for transfers between devices, from_tile(): return lax.ppermute(block, ('wave', 'tile'), pairs)  18.6 us
    ppermute x15, starting transfers between devices, partner(): lax.ppermute(block, 'wave', [(i, i ^ bit) for i in range(lax.axis_size('w...  13.6 us
    convert_element_type x3, other arithmetic, window_terms(): wave_imag.astype(jnp.bfloat16)  10.2 us
    another operation x6, other arithmetic, join_halves(): pair = jnp.stack([block, partner(block, 1)])  9.28 us
    dynamic_slice x6, local copies, waits for them, and re-layouts, join_halves(): high = lax.dynamic_index_in_dim(pair, 1 - core, 0, keepdims=False)  8.6 us
  transfers between devices with their start and end apart: 33, of which 17 were waited for; matrix products, arithmetic and copies ran while one was open for 9% of the time, Pallas kernels for 0%

profile of v3, /device:TPU:1, one launch (start us, length us, event | category | flops | bytes accessed | tf_op | source)
XLA Modules:
  0.0 402.7 jit_solution(6496257079015610414)
XLA Ops:
  11.2 3.4 collective-permute-start.3
  21.5 2.2 fusion.191
  34.4 5.1 %fusion.270 = (bf16[2,2,256,256]{3,2,0,1:T(8,128)(2,1)S(1)}, f32[2,2,256,256]{3,2,0,1:T(8,128)S(1)}, f32[2,2,256,256]{3,2,0,1:T(8,128)S(1)}, f32[2,2,256,256]{3,2,0,1:T(8,128)S(1)}) fusion(f32[2,256,256]{2,1,0:T(8,128)S(1)} %get-tuple-element.143, f32[2]{0:T(128)S(1)} %copy-done.22, f32[2,256,256]{2,1,0:T(8,128)} %copy.193, f32[2]{0:T(128)S(1)} %neg.15, ...), kind=kLoop, calls=%fused_computation.550 | loop fusion | flops 2621440 | bytes 5242896 | tf_op jit(solution)/shard_map/convert_element_type | solution.py:83
  53.6 2.6 collective-permute-done.4
  56.5 6.2 %collective-permute-start.7 = (f32[2,128,256]{2,1,0:T(8,128)S(1)}, f32[2,128,256]{2,1,0:T(8,128)S(1)}, u32[]{:S(2)}, u32[]{:S(2)}) collective-permute-start(f32[2,128,256]{2,1,0:T(8,128)S(1)} %get-tuple-element.137), channel_id=1, source_target_pairs={{0,9},{32,41},{64,73},{96,105},{128,137},{160,169},{192,201},{224,... | collective-permute-start | bytes 786440 | tf_op jit(solution)/shard_map/ppermute | solution.py:128
  62.6 3.7 collective-permute-start.6
  66.3 3.6 collective-permute-start.5
  70.0 3.8 collective-permute-done.6
  75.1 6.3 %collective-permute-done.8 = f32[2,128,256]{2,1,0:T(8,128)S(1)} collective-permute-done((f32[2,128,256]{2,1,0:T(8,128)S(1)}, f32[2,128,256]{2,1,0:T(8,128)S(1)}, u32[]{:S(2)}, u32[]{:S(2)}) %collective-permute-start.8) | collective-permute-done | bytes 262176 | tf_op jit(solution)/shard_map/ppermute | solution.py:132
  83.1 12.8 %collective-permute-done.9 = f32[2,128,256]{2,1,0:T(8,128)S(1)} collective-permute-done((f32[2,128,256]{2,1,0:T(8,128)S(1)}, f32[2,128,256]{2,1,0:T(8,128)S(1)}, u32[]{:S(2)}, u32[]{:S(2)}) %collective-permute-start.9) | collective-permute-done | bytes 262176 | tf_op jit(solution)/shard_map/ppermute | solution.py:132
  102.4 46.4 %all_to_all.18 = f32[32,1,128]{2,1,0:T(1,128)S(1)} all-to-all(f32[32,1,128]{2,1,0:T(1,128)S(1)} %broadcast_in_dim.8), channel_id=1, replica_groups=mesh['wave'=8,'tile'=32] {'tile'}, dimensions={0} | all-to-all | bytes 32768 | tf_op jit(solution)/shard_map/all_to_all | solution.py:110
  162.6 2.5 fusion.127
  166.5 2.3 copy.213
  178.3 5.4 %fusion.268 = (bf16[2,2,256,256]{3,2,0,1:T(8,128)(2,1)S(1)}, f32[2,2,256,256]{3,2,0,1:T(8,128)S(1)}, bf16[2,2,256,256]{3,2,0,1:T(8,128)(2,1)S(1)}, f32[2,2,256,256]{3,2,0,1:T(8,128)S(1)}) fusion(f32[2,256,256]{2,1,0:T(8,128)} %copy-done.1, f32[2]{0:T(128)S(1)} %copy-done.22, f32[2,256,256]{2,1,0:T(8,128)} %copy.217, f32[2]{0:T(128)S(1)} %neg.15, ...), kind=kLoop, calls=%fused_computation.549 | loop fusion | flops 3145728 | bytes 4718608 | tf_op jit(solution)/shard_map/convert_element_type | solution.py:83
  196.2 2.6 collective-permute-done.15
  199.1 2.3 collective-permute-start.18
  201.4 2.2 collective-permute-start.17
  206.9 5.6 %collective-permute-done.17 = f32[2,128,256]{2,1,0:T(8,128)S(1)} collective-permute-done((f32[2,128,256]{2,1,0:T(8,128)S(1)}, f32[2,128,256]{2,1,0:T(8,128)S(1)}, u32[]{:S(2)}, u32[]{:S(2)}) %collective-permute-start.17) | collective-permute-done | bytes 262176 | tf_op jit(solution)/shard_map/ppermute | solution.py:128
  212.9 6.9 %collective-permute-done.19 = f32[2,128,256]{2,1,0:T(8,128)S(1)} collective-permute-done((f32[2,128,256]{2,1,0:T(8,128)S(1)}, f32[2,128,256]{2,1,0:T(8,128)S(1)}, u32[]{:S(2)}, u32[]{:S(2)}) %collective-permute-start.19) | collective-permute-done | bytes 262176 | tf_op jit(solution)/shard_map/ppermute | solution.py:132
  219.9 14.7 %collective-permute-done.20 = f32[2,128,256]{2,1,0:T(8,128)S(1)} collective-permute-done((f32[2,128,256]{2,1,0:T(8,128)S(1)}, f32[2,128,256]{2,1,0:T(8,128)S(1)}, u32[]{:S(2)}, u32[]{:S(2)}) %collective-permute-start.20) | collective-permute-done | bytes 262176 | tf_op jit(solution)/shard_map/ppermute | solution.py:132
  247.4 36.4 %all_to_all.19 = f32[32,1,128]{2,1,0:T(1,128)S(1)} all-to-all(f32[32,1,128]{2,1,0:T(1,128)S(1)} %broadcast_in_dim.9), channel_id=1, replica_groups=mesh['wave'=8,'tile'=32] {'tile'}, dimensions={0} | all-to-all | bytes 32768 | tf_op jit(solution)/shard_map/all_to_all | solution.py:110
  287.1 2.3 collective-permute-start.25
  294.7 2.5 fusion.125
  297.2 2.3 copy.231
  299.5 2.3 copy.232
  309.6 4.6 %fusion.265 = (bf16[2,2,256,256]{3,2,0,1:T(8,128)(2,1)S(1)}, f32[2,2,256,256]{3,2,0,1:T(8,128)S(1)}, bf16[2,2,256,256]{3,2,0,1:T(8,128)(2,1)S(1)}, f32[2,2,256,256]{3,2,0,1:T(8,128)S(1)}) fusion(f32[2,256,256]{2,1,0:T(8,128)S(1)} %copy-done.2, f32[2]{0:T(128)S(1)} %copy-done.23, f32[2,256,256]{2,1,0:T(8,128)S(1)} %copy.236, f32[2]{0:T(128)S(1)} %copy-done.25, ...), kind=kLoop, calls=%fused_computation.547 | loop fusion | flops 3145728 | bytes 4718608 | tf_op jit(solution)/shard_map/convert_element_type | solution.py:83
  326.7 2.6 collective-permute-done.26
  329.5 2.3 collective-permute-start.29
  337.3 5.6 %collective-permute-done.28 = f32[2,128,256]{2,1,0:T(8,128)S(1)} collective-permute-done((f32[2,128,256]{2,1,0:T(8,128)S(1)}, f32[2,128,256]{2,1,0:T(8,128)S(1)}, u32[]{:S(2)}, u32[]{:S(2)}) %collective-permute-start.28) | collective-permute-done | bytes 262176 | tf_op jit(solution)/shard_map/ppermute | solution.py:128
  343.3 6.9 %collective-permute-done.30 = f32[2,128,256]{2,1,0:T(8,128)S(1)} collective-permute-done((f32[2,128,256]{2,1,0:T(8,128)S(1)}, f32[2,128,256]{2,1,0:T(8,128)S(1)}, u32[]{:S(2)}, u32[]{:S(2)}) %collective-permute-start.30) | collective-permute-done | bytes 262176 | tf_op jit(solution)/shard_map/ppermute | solution.py:132
  351.5 13.6 %collective-permute-done.31 = f32[2,128,256]{2,1,0:T(8,128)S(1)} collective-permute-done((f32[2,128,256]{2,1,0:T(8,128)S(1)}, f32[2,128,256]{2,1,0:T(8,128)S(1)}, u32[]{:S(2)}, u32[]{:S(2)}) %collective-permute-start.31) | collective-permute-done | bytes 262176 | tf_op jit(solution)/shard_map/ppermute | solution.py:132
  368.4 31.0 %all_to_all.20 = f32[32,1,128]{2,1,0:T(1,128)S(1)} all-to-all(f32[32,1,128]{2,1,0:T(1,128)S(1)} %broadcast_in_dim.10), channel_id=1, replica_groups=mesh['wave'=8,'tile'=32] {'tile'}, dimensions={0} | all-to-all | bytes 32768 | tf_op jit(solution)/shard_map/all_to_all | solution.py:110
  (278 shorter events, 145.3 us)
Async XLA Ops:
  1.1 9.2 %collective-permute-start.2 = (f32[128,256]{1,0:T(8,128)S(1)}, f32[128,256]{1,0:T(8,128)S(1)}, u32[]{:S(2)}, u32[]{:S(2)}) collective-permute-start(f32[128,256]{1,0:T(8,128)S(1)} %dynamic-slice_bitcast_fusion), channel_id=1, source_target_pairs={{9,0},{41,32},{73,64},{105,96},{137,128},{169,160},{201,192},{233,... | collective-permute-start | bytes 393224 | tf_op jit(solution)/shard_map/ppermute | solution.py:128
  2.4 7.9 %collective-permute-start.1 = (f32[128,256]{1,0:T(8,128)S(1)}, f32[128,256]{1,0:T(8,128)S(1)}, u32[]{:S(2)}, u32[]{:S(2)}) collective-permute-start(f32[128,256]{1,0:T(8,128)S(1)} %dynamic-slice_bitcast_fusion), channel_id=1, source_target_pairs={{8,0},{40,32},{72,64},{104,96},{136,128},{168,160},{200,192},{232,... | collective-permute-start | bytes 393224 | tf_op jit(solution)/shard_map/ppermute | solution.py:128
  3.7 6.8 %collective-permute-start = (f32[128,256]{1,0:T(8,128)S(1)}, f32[128,256]{1,0:T(8,128)S(1)}, u32[]{:S(2)}, u32[]{:S(2)}) collective-permute-start(f32[128,256]{1,0:T(8,128)S(1)} %dynamic-slice_bitcast_fusion), channel_id=1, source_target_pairs={{1,0},{33,32},{65,64},{97,96},{129,128},{161,160},{193,192},{225,2... | collective-permute-start | bytes 393224 | tf_op jit(solution)/shard_map/ppermute | solution.py:128
  11.2 10.2 %collective-permute-start.3 = (f32[3,128,256]{2,1,0:T(8,128)}, f32[3,128,256]{2,1,0:T(8,128)}, u32[]{:S(2)}, u32[]{:S(2)}) collective-permute-start(f32[3,128,256]{2,1,0:T(8,128)} %get-tuple-element.160), channel_id=1, source_target_pairs={{0,32},{32,0},{64,96},{96,64},{128,160},{160,128},{192,224},{224,1... | collective-permute-start | bytes 1179656 | tf_op jit(solution)/shard_map/ppermute | solution.py:132
  53.5 2.7 collective-permute-start.4
  56.5 13.5 %collective-permute-start.7 = (f32[2,128,256]{2,1,0:T(8,128)S(1)}, f32[2,128,256]{2,1,0:T(8,128)S(1)}, u32[]{:S(2)}, u32[]{:S(2)}) collective-permute-start(f32[2,128,256]{2,1,0:T(8,128)S(1)} %get-tuple-element.137), channel_id=1, source_target_pairs={{0,9},{32,41},{64,73},{96,105},{128,137},{160,169},{192,201},{224,... | collective-permute-start | bytes 786440 | tf_op jit(solution)/shard_map/ppermute | solution.py:128
  62.6 11.1 %collective-permute-start.6 = (f32[2,128,256]{2,1,0:T(8,128)S(1)}, f32[2,128,256]{2,1,0:T(8,128)S(1)}, u32[]{:S(2)}, u32[]{:S(2)}) collective-permute-start(f32[2,128,256]{2,1,0:T(8,128)S(1)} %get-tuple-element.138), channel_id=1, source_target_pairs={{0,8},{32,40},{64,72},{96,104},{128,136},{160,168},{192,200},{224,... | collective-permute-start | bytes 786440 | tf_op jit(solution)/shard_map/ppermute | solution.py:128
  66.3 8.6 %collective-permute-start.5 = (f32[2,128,256]{2,1,0:T(8,128)S(1)}, f32[2,128,256]{2,1,0:T(8,128)S(1)}, u32[]{:S(2)}, u32[]{:S(2)}) collective-permute-start(f32[2,128,256]{2,1,0:T(8,128)S(1)} %get-tuple-element.136), channel_id=1, source_target_pairs={{0,1},{32,33},{64,65},{96,97},{128,129},{160,161},{192,193},{224,2... | collective-permute-start | bytes 786440 | tf_op jit(solution)/shard_map/ppermute | solution.py:128
  75.0 6.4 %collective-permute-start.8 = (f32[2,128,256]{2,1,0:T(8,128)S(1)}, f32[2,128,256]{2,1,0:T(8,128)S(1)}, u32[]{:S(2)}, u32[]{:S(2)}) collective-permute-start(f32[2,128,256]{2,1,0:T(8,128)S(1)} %fusion.225), channel_id=1, source_target_pairs={{0,64},{32,96},{64,0},{96,32},{128,192},{160,224},{192,128},{224,1... | collective-permute-start | bytes 786440 | tf_op jit(solution)/shard_map/ppermute | solution.py:132
  81.4 14.6 %collective-permute-start.9 = (f32[2,128,256]{2,1,0:T(8,128)S(1)}, f32[2,128,256]{2,1,0:T(8,128)S(1)}, u32[]{:S(2)}, u32[]{:S(2)}) collective-permute-start(f32[2,128,256]{2,1,0:T(8,128)S(1)} %add.597), channel_id=1, source_target_pairs={{0,128},{32,160},{64,192},{96,224},{128,0},{160,32},{192,64},{224,... | collective-permute-start | bytes 786440 | tf_op jit(solution)/shard_map/ppermute | solution.py:132
  96.0 4.7 %collective-permute-start.10 = (f32[2,128,256]{2,1,0:T(8,128)S(1)}, f32[2,128,256]{2,1,0:T(8,128)S(1)}, u32[]{:S(2)}, u32[]{:S(2)}) collective-permute-start(f32[2,128,256]{2,1,0:T(8,128)S(1)} %add.598), channel_id=1, source_target_pairs={{0,32},{32,0},{64,96},{96,64},{128,160},{160,128},{192,224},{224,1... | collective-permute-start | bytes 786440 | tf_op jit(solution)/shard_map/ppermute | solution.py:132
  96.9 53.0 %collective-permute-start.13 = (f32[2,128,256]{2,1,0:T(8,128)S(1)}, f32[2,128,256]{2,1,0:T(8,128)}, u32[]{:S(2)}, u32[]{:S(2)}) collective-permute-start(f32[2,128,256]{2,1,0:T(8,128)S(1)} %add.598), channel_id=1, source_target_pairs={{9,0},{41,32},{73,64},{105,96},{137,128},{169,160},{201,192},{233,... | collective-permute-start | bytes 786440 | tf_op jit(solution)/shard_map/ppermute | solution.py:128
  98.1 51.7 %collective-permute-start.12 = (f32[2,128,256]{2,1,0:T(8,128)S(1)}, f32[2,128,256]{2,1,0:T(8,128)}, u32[]{:S(2)}, u32[]{:S(2)}) collective-permute-start(f32[2,128,256]{2,1,0:T(8,128)S(1)} %add.598), channel_id=1, source_target_pairs={{8,0},{40,32},{72,64},{104,96},{136,128},{168,160},{200,192},{232,... | collective-permute-start | bytes 786440 | tf_op jit(solution)/shard_map/ppermute | solution.py:128
  99.4 50.4 %collective-permute-start.11 = (f32[2,128,256]{2,1,0:T(8,128)S(1)}, f32[2,128,256]{2,1,0:T(8,128)}, u32[]{:S(2)}, u32[]{:S(2)}) collective-permute-start(f32[2,128,256]{2,1,0:T(8,128)S(1)} %add.598), channel_id=1, source_target_pairs={{1,0},{33,32},{65,64},{97,96},{129,128},{161,160},{193,192},{225,2... | collective-permute-start | bytes 786440 | tf_op jit(solution)/shard_map/ppermute | solution.py:128
  152.0 10.6 %collective-permute-start.14 = (f32[3,2,128,256]{3,2,1,0:T(8,128)}, f32[3,2,128,256]{3,2,1,0:T(8,128)}, u32[]{:S(2)}, u32[]{:S(2)}) collective-permute-start(f32[3,2,128,256]{3,2,1,0:T(8,128)} %maximum_add_fusion.1), channel_id=1, source_target_pairs={{0,32},{32,0},{64,96},{96,64},{128,160},{160,128},{192,224},{224,1... | collective-permute-start | bytes 2359304 | tf_op jit(solution)/shard_map/ppermute | solution.py:132
  196.1 2.7 collective-permute-start.15
  199.1 7.8 %collective-permute-start.18 = (f32[2,128,256]{2,1,0:T(8,128)S(1)}, f32[2,128,256]{2,1,0:T(8,128)S(1)}, u32[]{:S(2)}, u32[]{:S(2)}) collective-permute-start(f32[2,128,256]{2,1,0:T(8,128)S(1)} %get-tuple-element.127), channel_id=1, source_target_pairs={{0,9},{32,41},{64,73},{96,105},{128,137},{160,169},{192,201},{224,... | collective-permute-start | bytes 786440 | tf_op jit(solution)/shard_map/ppermute | solution.py:128
  201.4 11.1 %collective-permute-start.17 = (f32[2,128,256]{2,1,0:T(8,128)S(1)}, f32[2,128,256]{2,1,0:T(8,128)S(1)}, u32[]{:S(2)}, u32[]{:S(2)}) collective-permute-start(f32[2,128,256]{2,1,0:T(8,128)S(1)} %get-tuple-element.128), channel_id=1, source_target_pairs={{0,8},{32,40},{64,72},{96,104},{128,136},{160,168},{192,200},{224,... | collective-permute-start | bytes 786440 | tf_op jit(solution)/shard_map/ppermute | solution.py:128
  203.6 8.9 %collective-permute-start.16 = (f32[2,128,256]{2,1,0:T(8,128)S(1)}, f32[2,128,256]{2,1,0:T(8,128)S(1)}, u32[]{:S(2)}, u32[]{:S(2)}) collective-permute-start(f32[2,128,256]{2,1,0:T(8,128)S(1)} %get-tuple-element.126), channel_id=1, source_target_pairs={{0,1},{32,33},{64,65},{96,97},{128,129},{160,161},{192,193},{224,2... | collective-permute-start | bytes 786440 | tf_op jit(solution)/shard_map/ppermute | solution.py:128
  212.6 7.2 %collective-permute-start.19 = (f32[2,128,256]{2,1,0:T(8,128)S(1)}, f32[2,128,256]{2,1,0:T(8,128)S(1)}, u32[]{:S(2)}, u32[]{:S(2)}) collective-permute-start(f32[2,128,256]{2,1,0:T(8,128)S(1)} %fusion.221), channel_id=1, source_target_pairs={{0,64},{32,96},{64,0},{96,32},{128,192},{160,224},{192,128},{224,1... | collective-permute-start | bytes 786440 | tf_op jit(solution)/shard_map/ppermute | solution.py:132
  219.8 14.8 %collective-permute-start.20 = (f32[2,128,256]{2,1,0:T(8,128)S(1)}, f32[2,128,256]{2,1,0:T(8,128)S(1)}, u32[]{:S(2)}, u32[]{:S(2)}) collective-permute-start(f32[2,128,256]{2,1,0:T(8,128)S(1)} %add.640), channel_id=1, source_target_pairs={{0,128},{32,160},{64,192},{96,224},{128,0},{160,32},{192,64},{224,... | collective-permute-start | bytes 786440 | tf_op jit(solution)/shard_map/ppermute | solution.py:132
  235.4 4.4 %collective-permute-start.21 = (f32[2,128,256]{2,1,0:T(8,128)}, f32[2,128,256]{2,1,0:T(8,128)S(1)}, u32[]{:S(2)}, u32[]{:S(2)}) collective-permute-start(f32[2,128,256]{2,1,0:T(8,128)} %add.641), channel_id=1, source_target_pairs={{0,32},{32,0},{64,96},{96,64},{128,160},{160,128},{192,224},{224,1... | collective-permute-start | bytes 786440 | tf_op jit(solution)/shard_map/ppermute | solution.py:132
  235.9 49.1 %collective-permute-start.24 = (f32[2,128,256]{2,1,0:T(8,128)}, f32[2,128,256]{2,1,0:T(8,128)}, u32[]{:S(2)}, u32[]{:S(2)}) collective-permute-start(f32[2,128,256]{2,1,0:T(8,128)} %add.641), channel_id=1, source_target_pairs={{9,0},{41,32},{73,64},{105,96},{137,128},{169,160},{201,192},{233,... | collective-permute-start | bytes 786440 | tf_op jit(solution)/shard_map/ppermute | solution.py:128
  237.1 47.8 %collective-permute-start.23 = (f32[2,128,256]{2,1,0:T(8,128)}, f32[2,128,256]{2,1,0:T(8,128)}, u32[]{:S(2)}, u32[]{:S(2)}) collective-permute-start(f32[2,128,256]{2,1,0:T(8,128)} %add.641), channel_id=1, source_target_pairs={{8,0},{40,32},{72,64},{104,96},{136,128},{168,160},{200,192},{232,... | collective-permute-start | bytes 786440 | tf_op jit(solution)/shard_map/ppermute | solution.py:128
  238.4 46.6 %collective-permute-start.22 = (f32[2,128,256]{2,1,0:T(8,128)}, f32[2,128,256]{2,1,0:T(8,128)}, u32[]{:S(2)}, u32[]{:S(2)}) collective-permute-start(f32[2,128,256]{2,1,0:T(8,128)} %add.641), channel_id=1, source_target_pairs={{1,0},{33,32},{65,64},{97,96},{129,128},{161,160},{193,192},{225,2... | collective-permute-start | bytes 786440 | tf_op jit(solution)/shard_map/ppermute | solution.py:128
  287.1 7.6 %collective-permute-start.25 = (f32[3,2,128,256]{3,2,1,0:T(8,128)}, f32[3,2,128,256]{3,2,1,0:T(8,128)}, u32[]{:S(2)}, u32[]{:S(2)}) collective-permute-start(f32[3,2,128,256]{3,2,1,0:T(8,128)} %maximum_add_fusion.3), channel_id=1, source_target_pairs={{0,32},{32,0},{64,96},{96,64},{128,160},{160,128},{192,224},{224,1... | collective-permute-start | bytes 2359304 | tf_op jit(solution)/shard_map/ppermute | solution.py:132
  326.6 2.7 collective-permute-start.26
  329.5 7.8 %collective-permute-start.29 = (f32[2,128,256]{2,1,0:T(8,128)S(1)}, f32[2,128,256]{2,1,0:T(8,128)S(1)}, u32[]{:S(2)}, u32[]{:S(2)}) collective-permute-start(f32[2,128,256]{2,1,0:T(8,128)S(1)} %get-tuple-element.119), channel_id=1, source_target_pairs={{0,9},{32,41},{64,73},{96,105},{128,137},{160,169},{192,201},{224,... | collective-permute-start | bytes 786440 | tf_op jit(solution)/shard_map/ppermute | solution.py:128
  331.8 11.1 %collective-permute-start.28 = (f32[2,128,256]{2,1,0:T(8,128)S(1)}, f32[2,128,256]{2,1,0:T(8,128)S(1)}, u32[]{:S(2)}, u32[]{:S(2)}) collective-permute-start(f32[2,128,256]{2,1,0:T(8,128)S(1)} %get-tuple-element.120), channel_id=1, source_target_pairs={{0,8},{32,40},{64,72},{96,104},{128,136},{160,168},{192,200},{224,... | collective-permute-start | bytes 786440 | tf_op jit(solution)/shard_map/ppermute | solution.py:128
  334.1 8.9 %collective-permute-start.27 = (f32[2,128,256]{2,1,0:T(8,128)S(1)}, f32[2,128,256]{2,1,0:T(8,128)S(1)}, u32[]{:S(2)}, u32[]{:S(2)}) collective-permute-start(f32[2,128,256]{2,1,0:T(8,128)S(1)} %get-tuple-element.118), channel_id=1, source_target_pairs={{0,1},{32,33},{64,65},{96,97},{128,129},{160,161},{192,193},{224,2... | collective-permute-start | bytes 786440 | tf_op jit(solution)/shard_map/ppermute | solution.py:128
  343.1 7.1 %collective-permute-start.30 = (f32[2,128,256]{2,1,0:T(8,128)S(1)}, f32[2,128,256]{2,1,0:T(8,128)S(1)}, u32[]{:S(2)}, u32[]{:S(2)}) collective-permute-start(f32[2,128,256]{2,1,0:T(8,128)S(1)} %fusion.216), channel_id=1, source_target_pairs={{0,64},{32,96},{64,0},{96,32},{128,192},{160,224},{192,128},{224,1... | collective-permute-start | bytes 786440 | tf_op jit(solution)/shard_map/ppermute | solution.py:132
  350.2 14.8 %collective-permute-start.31 = (f32[2,128,256]{2,1,0:T(8,128)S(1)}, f32[2,128,256]{2,1,0:T(8,128)S(1)}, u32[]{:S(2)}, u32[]{:S(2)}) collective-permute-start(f32[2,128,256]{2,1,0:T(8,128)S(1)} %add.683), channel_id=1, source_target_pairs={{0,128},{32,160},{64,192},{96,224},{128,0},{160,32},{192,64},{224,... | collective-permute-start | bytes 786440 | tf_op jit(solution)/shard_map/ppermute | solution.py:132
  (39 other events, 595.2 us)

commit v4 on v2

--- a/solution.py
+++ b/solution.py
@@ -133,10 +133,10 @@
 
 
 def z_sum(block):
-    bit = 2
-    while bit < lax.axis_size("wave"):
+    bit = lax.axis_size("wave") // 2
+    while bit >= 2:
         block = block + partner(block, bit)
-        bit *= 2
+        bit //= 2
     return block
 
 

time: 379 us -> 378 us (level)
  starting transfers between devices: 51.6 us -> 58.9 us
  blocking collectives: 107 us -> 102 us
    ppermute x15, starting transfers between devices: 15.8 us -> 23.1 us  [partner(): lax.ppermute(block, 'wave', [(i, i ^ bit) for i in range(lax.axis_size('w...]
    all_to_all x3, blocking collectives: 107 us -> 102 us  [tile_max(): gathered = lax.all_to_all(spread, 'tile', 0, 0, tiled=True)]
where the time goes in v4:
time: 378 us; the launch traced here: 374 us
  blocking collectives  102 us (27%)
  waiting for transfers between devices  90.9 us (24%)
  other arithmetic  61.1 us (16%)
  starting transfers between devices  58.9 us (16%)
  local copies, waits for them, and re-layouts  32.1 us (8%)
  matrix products  23.4 us (6%)
  between operations  5.12 us (1%)
    all_to_all x3, blocking collectives, tile_max(): gathered = lax.all_to_all(spread, 'tile', 0, 0, tiled=True)  102 us
    ppermute x15, waiting for transfers between devices, partner(): lax.ppermute(block, 'wave', [(i, i ^ bit) for i in range(lax.axis_size('w...  64.9 us
    ppermute x18, starting transfers between devices, from_tile(): return lax.ppermute(block, ('wave', 'tile'), pairs)  35.8 us
    ppermute x18, waiting for transfers between devices, from_tile(): return lax.ppermute(block, ('wave', 'tile'), pairs)  26 us
    ppermute x15, starting transfers between devices, partner(): lax.ppermute(block, 'wave', [(i, i ^ bit) for i in range(lax.axis_size('w...  23.1 us
    convert_element_type x3, other arithmetic, window_terms(): wave_imag.astype(jnp.bfloat16)  10.1 us
    unnamed x89, local copies, waits for them, and re-layouts  9.27 us
    another operation x20, other arithmetic  8.74 us
  transfers between devices with their start and end apart: 33, of which 19 were waited for; matrix products, arithmetic and copies ran while one was open for 8% of the time, Pallas kernels for 0%

profile of v4, /device:TPU:1, one launch (start us, length us, event | category | flops | bytes accessed | tf_op | source)
XLA Modules:
  0.0 373.6 jit_solution(8488049549142363734)
XLA Ops:
  10.4 2.2 collective-permute-done.2
  12.6 4.0 %collective-permute-start.3 = (f32[3,128,256]{1,2,0:T(8,128)S(1)}, f32[3,128,256]{1,2,0:T(8,128)}, u32[]{:S(2)}, u32[]{:S(2)}) collective-permute-start(f32[3,128,256]{1,2,0:T(8,128)S(1)} %pad_maximum_fusion.22), channel_id=1, source_target_pairs={{0,32},{32,0},{64,96},{96,64},{128,160},{160,128},{192,224},{224,1... | collective-permute-start | bytes 1179656 | tf_op jit(solution)/shard_map/ppermute | solution.py:132
  31.0 5.1 %fusion.272 = (bf16[2,2,256,256]{3,2,0,1:T(8,128)(2,1)S(1)}, f32[2,2,256,256]{3,2,0,1:T(8,128)S(1)}, f32[2,2,256,256]{3,2,0,1:T(8,128)S(1)}, f32[2,2,256,256]{3,2,0,1:T(8,128)S(1)}) fusion(f32[2,256,256]{2,1,0:T(8,128)S(1)} %get-tuple-element.143, f32[2]{0:T(128)S(1)} %copy-done.30, f32[2,256,256]{2,1,0:T(8,128)} %copy.188, f32[2]{0:T(128)S(1)} %neg.15, ...), kind=kLoop, calls=%fused_computation.532 | loop fusion | flops 2621440 | bytes 5242896 | tf_op jit(solution)/shard_map/convert_element_type | solution.py:83
  48.5 2.6 collective-permute-done.4
  51.3 2.5 collective-permute-start.5
  53.7 4.3 %collective-permute-start.6 = (f32[2,128,256]{1,2,0:T(8,128)S(1)}, f32[2,128,256]{1,2,0:T(8,128)S(1)}, u32[]{:S(2)}, u32[]{:S(2)}) collective-permute-start(f32[2,128,256]{1,2,0:T(8,128)S(1)} %get-tuple-element.138), channel_id=1, source_target_pairs={{0,8},{32,40},{64,72},{96,104},{128,136},{160,168},{192,200},{224,... | collective-permute-start | bytes 786440 | tf_op jit(solution)/shard_map/ppermute | solution.py:128
  58.0 4.1 %collective-permute-start.7 = (f32[2,128,256]{1,2,0:T(8,128)S(1)}, f32[2,128,256]{1,2,0:T(8,128)S(1)}, u32[]{:S(2)}, u32[]{:S(2)}) collective-permute-start(f32[2,128,256]{1,2,0:T(8,128)S(1)} %get-tuple-element.137), channel_id=1, source_target_pairs={{0,9},{32,41},{64,73},{96,105},{128,137},{160,169},{192,201},{224,... | collective-permute-start | bytes 786440 | tf_op jit(solution)/shard_map/ppermute | solution.py:128
  63.2 5.6 %collective-permute-done.7 = f32[2,128,256]{1,2,0:T(8,128)S(1)} collective-permute-done((f32[2,128,256]{1,2,0:T(8,128)S(1)}, f32[2,128,256]{1,2,0:T(8,128)S(1)}, u32[]{:S(2)}, u32[]{:S(2)}) %collective-permute-start.7) | collective-permute-done | bytes 262176 | tf_op jit(solution)/shard_map/ppermute | solution.py:128
  70.7 12.2 %collective-permute-done.8 = f32[2,128,256]{1,2,0:T(8,128)S(1)} collective-permute-done((f32[2,128,256]{1,2,0:T(8,128)S(1)}, f32[2,128,256]{1,2,0:T(8,128)S(1)}, u32[]{:S(2)}, u32[]{:S(2)}) %collective-permute-start.8) | collective-permute-done | bytes 262176 | tf_op jit(solution)/shard_map/ppermute | solution.py:132
  83.7 6.0 %collective-permute-done.9 = f32[2,128,256]{1,2,0:T(8,128)S(1)} collective-permute-done((f32[2,128,256]{1,2,0:T(8,128)S(1)}, f32[2,128,256]{1,2,0:T(8,128)S(1)}, u32[]{:S(2)}, u32[]{:S(2)}) %collective-permute-start.9) | collective-permute-done | bytes 262176 | tf_op jit(solution)/shard_map/ppermute | solution.py:132
  98.8 38.6 %all_to_all.18 = f32[32,1,128]{2,1,0:T(1,128)} all-to-all(f32[32,1,128]{2,1,0:T(1,128)S(1)} %broadcast_in_dim.8), channel_id=1, replica_groups=mesh['wave'=8,'tile'=32] {'tile'}, dimensions={0} | all-to-all | bytes 32768 | tf_op jit(solution)/shard_map/all_to_all | solution.py:110
  141.5 2.1 collective-permute-start.14
  162.0 5.4 %fusion.270 = (bf16[2,2,256,256]{3,2,0,1:T(8,128)(2,1)S(1)}, f32[2,2,256,256]{3,2,0,1:T(8,128)S(1)}, bf16[2,2,256,256]{3,2,0,1:T(8,128)(2,1)S(1)}, f32[2,2,256,256]{3,2,0,1:T(8,128)S(1)}) fusion(f32[2,256,256]{2,1,0:T(8,128)} %copy-done.1, f32[2]{0:T(128)S(1)} %copy-done.30, f32[2,256,256]{2,1,0:T(8,128)} %copy.211, f32[2]{0:T(128)S(1)} %neg.15, ...), kind=kLoop, calls=%fused_computation.531 | loop fusion | flops 3145728 | bytes 4718608 | tf_op jit(solution)/shard_map/convert_element_type | solution.py:83
  178.7 2.6 collective-permute-done.15
  181.5 2.4 collective-permute-start.16
  183.9 2.1 collective-permute-start.17
  186.0 2.1 collective-permute-start.18
  191.2 5.6 %collective-permute-done.18 = f32[2,128,256]{1,2,0:T(8,128)S(1)} collective-permute-done((f32[2,128,256]{1,2,0:T(8,128)S(1)}, f32[2,128,256]{1,2,0:T(8,128)S(1)}, u32[]{:S(2)}, u32[]{:S(2)}) %collective-permute-start.18) | collective-permute-done | bytes 262176 | tf_op jit(solution)/shard_map/ppermute | solution.py:128
  196.8 3.2 collective-permute-start.19
  200.0 11.2 %collective-permute-done.19 = f32[2,128,256]{1,2,0:T(8,128)S(1)} collective-permute-done((f32[2,128,256]{1,2,0:T(8,128)S(1)}, f32[2,128,256]{1,2,0:T(8,128)S(1)}, u32[]{:S(2)}, u32[]{:S(2)}) %collective-permute-start.19) | collective-permute-done | bytes 262176 | tf_op jit(solution)/shard_map/ppermute | solution.py:132
  213.0 5.2 %collective-permute-done.20 = f32[2,128,256]{1,2,0:T(8,128)S(1)} collective-permute-done((f32[2,128,256]{1,2,0:T(8,128)S(1)}, f32[2,128,256]{1,2,0:T(8,128)S(1)}, u32[]{:S(2)}, u32[]{:S(2)}) %collective-permute-start.20) | collective-permute-done | bytes 262176 | tf_op jit(solution)/shard_map/ppermute | solution.py:132
  227.9 36.3 %all_to_all.19 = f32[32,1,128]{2,1,0:T(1,128)S(1)} all-to-all(f32[32,1,128]{2,1,0:T(1,128)S(1)} %broadcast_in_dim.9), channel_id=1, replica_groups=mesh['wave'=8,'tile'=32] {'tile'}, dimensions={0} | all-to-all | bytes 32768 | tf_op jit(solution)/shard_map/all_to_all | solution.py:110
  267.7 2.3 collective-permute-start.25
  282.8 4.5 %fusion.267 = (bf16[2,2,256,256]{3,2,0,1:T(8,128)(2,1)S(1)}, f32[2,2,256,256]{3,2,0,1:T(8,128)S(1)}, bf16[2,2,256,256]{3,2,0,1:T(8,128)(2,1)S(1)}, f32[2,2,256,256]{3,2,0,1:T(8,128)S(1)}) fusion(f32[2,256,256]{2,1,0:T(8,128)S(1)} %copy-done.2, f32[2]{0:T(128)S(1)} %copy-done.31, f32[2,256,256]{2,1,0:T(8,128)S(1)} %copy.229, f32[2]{0:T(128)S(1)} %copy-done.33, ...), kind=kLoop, calls=%fused_computation.529 | loop fusion | flops 3145728 | bytes 4718608 | tf_op jit(solution)/shard_map/convert_element_type | solution.py:83
  298.7 2.6 collective-permute-done.26
  301.5 2.2 collective-permute-start.27
  303.7 2.3 collective-permute-start.28
  306.0 2.2 collective-permute-start.29
  311.2 5.6 %collective-permute-done.29 = f32[2,128,256]{1,2,0:T(8,128)S(1)} collective-permute-done((f32[2,128,256]{1,2,0:T(8,128)S(1)}, f32[2,128,256]{1,2,0:T(8,128)S(1)}, u32[]{:S(2)}, u32[]{:S(2)}) %collective-permute-start.29) | collective-permute-done | bytes 262176 | tf_op jit(solution)/shard_map/ppermute | solution.py:128
  317.6 13.8 %collective-permute-done.30 = f32[2,128,256]{1,2,0:T(8,128)S(1)} collective-permute-done((f32[2,128,256]{1,2,0:T(8,128)S(1)}, f32[2,128,256]{1,2,0:T(8,128)S(1)}, u32[]{:S(2)}, u32[]{:S(2)}) %collective-permute-start.30) | collective-permute-done | bytes 262176 | tf_op jit(solution)/shard_map/ppermute | solution.py:132
  331.5 7.4 %collective-permute-done.31 = f32[2,128,256]{1,2,0:T(8,128)S(1)} collective-permute-done((f32[2,128,256]{1,2,0:T(8,128)S(1)}, f32[2,128,256]{1,2,0:T(8,128)S(1)}, u32[]{:S(2)}, u32[]{:S(2)}) %collective-permute-start.31) | collective-permute-done | bytes 262176 | tf_op jit(solution)/shard_map/ppermute | solution.py:132
  342.8 27.2 %all_to_all.20 = f32[32,1,128]{2,1,0:T(1,128)S(1)} all-to-all(f32[32,1,128]{2,1,0:T(1,128)S(1)} %broadcast_in_dim.10), channel_id=1, replica_groups=mesh['wave'=8,'tile'=32] {'tile'}, dimensions={0} | all-to-all | bytes 32768 | tf_op jit(solution)/shard_map/all_to_all | solution.py:110
  (274 shorter events, 132.9 us)
Async XLA Ops:
  1.1 9.2 %collective-permute-start = (f32[128,256]{0,1:T(8,128)S(1)}, f32[128,256]{0,1:T(8,128)S(1)}, u32[]{:S(2)}, u32[]{:S(2)}) collective-permute-start(f32[128,256]{0,1:T(8,128)S(1)} %bitcast.365), channel_id=1, source_target_pairs={{1,0},{33,32},{65,64},{97,96},{129,128},{161,160},{193,192},{225,2... | collective-permute-start | bytes 393224 | tf_op jit(solution)/shard_map/ppermute | solution.py:128
  2.4 8.0 %collective-permute-start.1 = (f32[128,256]{0,1:T(8,128)S(1)}, f32[128,256]{0,1:T(8,128)S(1)}, u32[]{:S(2)}, u32[]{:S(2)}) collective-permute-start(f32[128,256]{0,1:T(8,128)S(1)} %bitcast.366), channel_id=1, source_target_pairs={{8,0},{40,32},{72,64},{104,96},{136,128},{168,160},{200,192},{232,... | collective-permute-start | bytes 393224 | tf_op jit(solution)/shard_map/ppermute | solution.py:128
  3.7 8.8 %collective-permute-start.2 = (f32[128,256]{0,1:T(8,128)S(1)}, f32[128,256]{0,1:T(8,128)S(1)}, u32[]{:S(2)}, u32[]{:S(2)}) collective-permute-start(f32[128,256]{0,1:T(8,128)S(1)} %bitcast.367), channel_id=1, source_target_pairs={{9,0},{41,32},{73,64},{105,96},{137,128},{169,160},{201,192},{233,... | collective-permute-start | bytes 393224 | tf_op jit(solution)/shard_map/ppermute | solution.py:128
  12.6 11.5 %collective-permute-start.3 = (f32[3,128,256]{1,2,0:T(8,128)S(1)}, f32[3,128,256]{1,2,0:T(8,128)}, u32[]{:S(2)}, u32[]{:S(2)}) collective-permute-start(f32[3,128,256]{1,2,0:T(8,128)S(1)} %pad_maximum_fusion.22), channel_id=1, source_target_pairs={{0,32},{32,0},{64,96},{96,64},{128,160},{160,128},{192,224},{224,1... | collective-permute-start | bytes 1179656 | tf_op jit(solution)/shard_map/ppermute | solution.py:132
  48.3 2.7 collective-permute-start.4
  51.3 10.9 %collective-permute-start.5 = (f32[2,128,256]{1,2,0:T(8,128)S(1)}, f32[2,128,256]{1,2,0:T(8,128)S(1)}, u32[]{:S(2)}, u32[]{:S(2)}) collective-permute-start(f32[2,128,256]{1,2,0:T(8,128)S(1)} %get-tuple-element.136), channel_id=1, source_target_pairs={{0,1},{32,33},{64,65},{96,97},{128,129},{160,161},{192,193},{224,2... | collective-permute-start | bytes 786440 | tf_op jit(solution)/shard_map/ppermute | solution.py:128
  53.7 9.5 %collective-permute-start.6 = (f32[2,128,256]{1,2,0:T(8,128)S(1)}, f32[2,128,256]{1,2,0:T(8,128)S(1)}, u32[]{:S(2)}, u32[]{:S(2)}) collective-permute-start(f32[2,128,256]{1,2,0:T(8,128)S(1)} %get-tuple-element.138), channel_id=1, source_target_pairs={{0,8},{32,40},{64,72},{96,104},{128,136},{160,168},{192,200},{224,... | collective-permute-start | bytes 786440 | tf_op jit(solution)/shard_map/ppermute | solution.py:128
  58.0 10.8 %collective-permute-start.7 = (f32[2,128,256]{1,2,0:T(8,128)S(1)}, f32[2,128,256]{1,2,0:T(8,128)S(1)}, u32[]{:S(2)}, u32[]{:S(2)}) collective-permute-start(f32[2,128,256]{1,2,0:T(8,128)S(1)} %get-tuple-element.137), channel_id=1, source_target_pairs={{0,9},{32,41},{64,73},{96,105},{128,137},{160,169},{192,201},{224,... | collective-permute-start | bytes 786440 | tf_op jit(solution)/shard_map/ppermute | solution.py:128
  68.9 14.1 %collective-permute-start.8 = (f32[2,128,256]{1,2,0:T(8,128)S(1)}, f32[2,128,256]{1,2,0:T(8,128)S(1)}, u32[]{:S(2)}, u32[]{:S(2)}) collective-permute-start(f32[2,128,256]{1,2,0:T(8,128)S(1)} %fusion.228), channel_id=1, source_target_pairs={{0,128},{32,160},{64,192},{96,224},{128,0},{160,32},{192,64},{224,... | collective-permute-start | bytes 786440 | tf_op jit(solution)/shard_map/ppermute | solution.py:132
  83.0 6.7 %collective-permute-start.9 = (f32[2,128,256]{1,2,0:T(8,128)S(1)}, f32[2,128,256]{1,2,0:T(8,128)S(1)}, u32[]{:S(2)}, u32[]{:S(2)}) collective-permute-start(f32[2,128,256]{1,2,0:T(8,128)S(1)} %add.553), channel_id=1, source_target_pairs={{0,64},{32,96},{64,0},{96,32},{128,192},{160,224},{192,128},{224,1... | collective-permute-start | bytes 786440 | tf_op jit(solution)/shard_map/ppermute | solution.py:132
  90.5 6.0 %collective-permute-start.10 = (f32[2,128,256]{1,2,0:T(8,128)}, f32[2,128,256]{1,2,0:T(8,128)S(1)}, u32[]{:S(2)}, u32[]{:S(2)}) collective-permute-start(f32[2,128,256]{1,2,0:T(8,128)} %add.554), channel_id=1, source_target_pairs={{0,32},{32,0},{64,96},{96,64},{128,160},{160,128},{192,224},{224,1... | collective-permute-start | bytes 786440 | tf_op jit(solution)/shard_map/ppermute | solution.py:132
  92.6 46.8 %collective-permute-start.11 = (f32[2,128,256]{1,2,0:T(8,128)}, f32[2,128,256]{1,2,0:T(8,128)S(1)}, u32[]{:S(2)}, u32[]{:S(2)}) collective-permute-start(f32[2,128,256]{1,2,0:T(8,128)} %add.554), channel_id=1, source_target_pairs={{1,0},{33,32},{65,64},{97,96},{129,128},{161,160},{193,192},{225,2... | collective-permute-start | bytes 786440 | tf_op jit(solution)/shard_map/ppermute | solution.py:128
  93.8 45.5 %collective-permute-start.12 = (f32[2,128,256]{1,2,0:T(8,128)}, f32[2,128,256]{1,2,0:T(8,128)S(1)}, u32[]{:S(2)}, u32[]{:S(2)}) collective-permute-start(f32[2,128,256]{1,2,0:T(8,128)} %add.554), channel_id=1, source_target_pairs={{8,0},{40,32},{72,64},{104,96},{136,128},{168,160},{200,192},{232,... | collective-permute-start | bytes 786440 | tf_op jit(solution)/shard_map/ppermute | solution.py:128
  95.1 44.2 %collective-permute-start.13 = (f32[2,128,256]{1,2,0:T(8,128)}, f32[2,128,256]{1,2,0:T(8,128)}, u32[]{:S(2)}, u32[]{:S(2)}) collective-permute-start(f32[2,128,256]{1,2,0:T(8,128)} %add.554), channel_id=1, source_target_pairs={{9,0},{41,32},{73,64},{105,96},{137,128},{169,160},{201,192},{233,... | collective-permute-start | bytes 786440 | tf_op jit(solution)/shard_map/ppermute | solution.py:128
  141.5 9.8 %collective-permute-start.14 = (f32[3,2,128,256]{2,3,1,0:T(8,128)}, f32[3,2,128,256]{2,3,1,0:T(8,128)}, u32[]{:S(2)}, u32[]{:S(2)}) collective-permute-start(f32[3,2,128,256]{2,3,1,0:T(8,128)} %maximum_add_fusion), channel_id=1, source_target_pairs={{0,32},{32,0},{64,96},{96,64},{128,160},{160,128},{192,224},{224,1... | collective-permute-start | bytes 2359304 | tf_op jit(solution)/shard_map/ppermute | solution.py:132
  178.4 3.0 collective-permute-start.15
  181.5 7.8 %collective-permute-start.16 = (f32[2,128,256]{1,2,0:T(8,128)S(1)}, f32[2,128,256]{1,2,0:T(8,128)S(1)}, u32[]{:S(2)}, u32[]{:S(2)}) collective-permute-start(f32[2,128,256]{1,2,0:T(8,128)S(1)} %get-tuple-element.126), channel_id=1, source_target_pairs={{0,1},{32,33},{64,65},{96,97},{128,129},{160,161},{192,193},{224,2... | collective-permute-start | bytes 786440 | tf_op jit(solution)/shard_map/ppermute | solution.py:128
  183.9 7.3 %collective-permute-start.17 = (f32[2,128,256]{1,2,0:T(8,128)S(1)}, f32[2,128,256]{1,2,0:T(8,128)S(1)}, u32[]{:S(2)}, u32[]{:S(2)}) collective-permute-start(f32[2,128,256]{1,2,0:T(8,128)S(1)} %get-tuple-element.128), channel_id=1, source_target_pairs={{0,8},{32,40},{64,72},{96,104},{128,136},{160,168},{192,200},{224,... | collective-permute-start | bytes 786440 | tf_op jit(solution)/shard_map/ppermute | solution.py:128
  186.0 10.8 %collective-permute-start.18 = (f32[2,128,256]{1,2,0:T(8,128)S(1)}, f32[2,128,256]{1,2,0:T(8,128)S(1)}, u32[]{:S(2)}, u32[]{:S(2)}) collective-permute-start(f32[2,128,256]{1,2,0:T(8,128)S(1)} %get-tuple-element.127), channel_id=1, source_target_pairs={{0,9},{32,41},{64,73},{96,105},{128,137},{160,169},{192,201},{224,... | collective-permute-start | bytes 786440 | tf_op jit(solution)/shard_map/ppermute | solution.py:128
  196.8 14.4 %collective-permute-start.19 = (f32[2,128,256]{1,2,0:T(8,128)S(1)}, f32[2,128,256]{1,2,0:T(8,128)S(1)}, u32[]{:S(2)}, u32[]{:S(2)}) collective-permute-start(f32[2,128,256]{1,2,0:T(8,128)S(1)} %fusion.224), channel_id=1, source_target_pairs={{0,128},{32,160},{64,192},{96,224},{128,0},{160,32},{192,64},{224,... | collective-permute-start | bytes 786440 | tf_op jit(solution)/shard_map/ppermute | solution.py:132
  211.3 6.9 %collective-permute-start.20 = (f32[2,128,256]{1,2,0:T(8,128)S(1)}, f32[2,128,256]{1,2,0:T(8,128)S(1)}, u32[]{:S(2)}, u32[]{:S(2)}) collective-permute-start(f32[2,128,256]{1,2,0:T(8,128)S(1)} %add.594), channel_id=1, source_target_pairs={{0,64},{32,96},{64,0},{96,32},{128,192},{160,224},{192,128},{224,1... | collective-permute-start | bytes 786440 | tf_op jit(solution)/shard_map/ppermute | solution.py:132
  218.9 6.0 %collective-permute-start.21 = (f32[2,128,256]{1,2,0:T(8,128)}, f32[2,128,256]{1,2,0:T(8,128)S(1)}, u32[]{:S(2)}, u32[]{:S(2)}) collective-permute-start(f32[2,128,256]{1,2,0:T(8,128)} %add.595), channel_id=1, source_target_pairs={{0,32},{32,0},{64,96},{96,64},{128,160},{160,128},{192,224},{224,1... | collective-permute-start | bytes 786440 | tf_op jit(solution)/shard_map/ppermute | solution.py:132
  221.0 44.6 %collective-permute-start.22 = (f32[2,128,256]{1,2,0:T(8,128)}, f32[2,128,256]{1,2,0:T(8,128)}, u32[]{:S(2)}, u32[]{:S(2)}) collective-permute-start(f32[2,128,256]{1,2,0:T(8,128)} %add.595), channel_id=1, source_target_pairs={{1,0},{33,32},{65,64},{97,96},{129,128},{161,160},{193,192},{225,2... | collective-permute-start | bytes 786440 | tf_op jit(solution)/shard_map/ppermute | solution.py:128
  222.3 43.3 %collective-permute-start.23 = (f32[2,128,256]{1,2,0:T(8,128)}, f32[2,128,256]{1,2,0:T(8,128)}, u32[]{:S(2)}, u32[]{:S(2)}) collective-permute-start(f32[2,128,256]{1,2,0:T(8,128)} %add.595), channel_id=1, source_target_pairs={{8,0},{40,32},{72,64},{104,96},{136,128},{168,160},{200,192},{232,... | collective-permute-start | bytes 786440 | tf_op jit(solution)/shard_map/ppermute | solution.py:128
  223.6 42.0 %collective-permute-start.24 = (f32[2,128,256]{1,2,0:T(8,128)}, f32[2,128,256]{1,2,0:T(8,128)}, u32[]{:S(2)}, u32[]{:S(2)}) collective-permute-start(f32[2,128,256]{1,2,0:T(8,128)} %add.595), channel_id=1, source_target_pairs={{9,0},{41,32},{73,64},{105,96},{137,128},{169,160},{201,192},{233,... | collective-permute-start | bytes 786440 | tf_op jit(solution)/shard_map/ppermute | solution.py:128
  267.7 6.5 %collective-permute-start.25 = (f32[3,2,128,256]{2,3,1,0:T(8,128)}, f32[3,2,128,256]{2,3,1,0:T(8,128)}, u32[]{:S(2)}, u32[]{:S(2)}) collective-permute-start(f32[3,2,128,256]{2,3,1,0:T(8,128)} %maximum_add_fusion.1), channel_id=1, source_target_pairs={{0,32},{32,0},{64,96},{96,64},{128,160},{160,128},{192,224},{224,1... | collective-permute-start | bytes 2359304 | tf_op jit(solution)/shard_map/ppermute | solution.py:132
  298.3 3.0 collective-permute-start.26
  301.5 7.7 %collective-permute-start.27 = (f32[2,128,256]{1,2,0:T(8,128)S(1)}, f32[2,128,256]{1,2,0:T(8,128)S(1)}, u32[]{:S(2)}, u32[]{:S(2)}) collective-permute-start(f32[2,128,256]{1,2,0:T(8,128)S(1)} %get-tuple-element.118), channel_id=1, source_target_pairs={{0,1},{32,33},{64,65},{96,97},{128,129},{160,161},{192,193},{224,2... | collective-permute-start | bytes 786440 | tf_op jit(solution)/shard_map/ppermute | solution.py:128
  303.7 7.4 %collective-permute-start.28 = (f32[2,128,256]{1,2,0:T(8,128)S(1)}, f32[2,128,256]{1,2,0:T(8,128)S(1)}, u32[]{:S(2)}, u32[]{:S(2)}) collective-permute-start(f32[2,128,256]{1,2,0:T(8,128)S(1)} %get-tuple-element.120), channel_id=1, source_target_pairs={{0,8},{32,40},{64,72},{96,104},{128,136},{160,168},{192,200},{224,... | collective-permute-start | bytes 786440 | tf_op jit(solution)/shard_map/ppermute | solution.py:128
  306.0 10.8 %collective-permute-start.29 = (f32[2,128,256]{1,2,0:T(8,128)S(1)}, f32[2,128,256]{1,2,0:T(8,128)S(1)}, u32[]{:S(2)}, u32[]{:S(2)}) collective-permute-start(f32[2,128,256]{1,2,0:T(8,128)S(1)} %get-tuple-element.119), channel_id=1, source_target_pairs={{0,9},{32,41},{64,73},{96,105},{128,137},{160,169},{192,201},{224,... | collective-permute-start | bytes 786440 | tf_op jit(solution)/shard_map/ppermute | solution.py:128
  316.9 14.5 %collective-permute-start.30 = (f32[2,128,256]{1,2,0:T(8,128)S(1)}, f32[2,128,256]{1,2,0:T(8,128)S(1)}, u32[]{:S(2)}, u32[]{:S(2)}) collective-permute-start(f32[2,128,256]{1,2,0:T(8,128)S(1)} %fusion.219), channel_id=1, source_target_pairs={{0,128},{32,160},{64,192},{96,224},{128,0},{160,32},{192,64},{224,... | collective-permute-start | bytes 786440 | tf_op jit(solution)/shard_map/ppermute | solution.py:132
  331.4 7.5 %collective-permute-start.31 = (f32[2,128,256]{1,2,0:T(8,128)S(1)}, f32[2,128,256]{1,2,0:T(8,128)S(1)}, u32[]{:S(2)}, u32[]{:S(2)}) collective-permute-start(f32[2,128,256]{1,2,0:T(8,128)S(1)} %add.635), channel_id=1, source_target_pairs={{0,64},{32,96},{64,0},{96,32},{128,192},{160,224},{192,128},{224,1... | collective-permute-start | bytes 786440 | tf_op jit(solution)/shard_map/ppermute | solution.py:132
  (45 other events, 553.9 us)
